TPU v7x, 32 devices: a whole 2x2x4 slice. The times are simulated.
32 devices in a mesh: fsdp: 8 (over y, x, core), dp: 4 (over z).
Axes of the slice: x: 2, y: 2, z: 4, core: 2. Of those that a mesh axis runs over, the one named last changes fastest.
Arguments:
- tokens: bfloat16 [131072, 1024], P(('fsdp', 'dp')), may hold values from -6 to 6
- cotangent: bfloat16 [131072, 1024], P(('fsdp', 'dp')), may hold values from -6 to 6
- lengths: int32 [256], P(('fsdp', 'dp')), may hold values from 8 to 2048, as said below
- selected: int32 [16384], P(('fsdp', 'dp')), may hold values from 0 to 4095, as said below
- attn_in: bfloat16 [1024, 3072], P('fsdp'), may hold values from -0.1875 to 0.1875
- attn_out: bfloat16 [1024, 1024], P('fsdp'), may hold values from -0.75 to 0.75
- mlp_in: bfloat16 [1024, 4096], P('fsdp'), may hold values from -0.1875 to 0.1875
- mlp_out: bfloat16 [4096, 1024], P('fsdp'), may hold values from -0.09375 to 0.09375
- norm_attn: bfloat16 [1024], P('fsdp'), may hold values from 0.5 to 1.5
- norm_mlp: bfloat16 [1024], P('fsdp'), may hold values from 0.5 to 1.5
- router: bfloat16 [1024], replicated, may hold values from -0.1875 to 0.1875
Outputs:
- output: bfloat16 [131072, 1024], P(('fsdp', 'dp'))
- grad_tokens: bfloat16 [131072, 1024], P(('fsdp', 'dp'))
- grad_attn_in: float32 [1024, 3072], P('fsdp')
- grad_attn_out: float32 [1024, 1024], P('fsdp')
- grad_mlp_in: float32 [1024, 4096], P('fsdp')
- grad_mlp_out: float32 [4096, 1024], P('fsdp')
- grad_norm_attn: float32 [1024], P('fsdp')
- grad_norm_mlp: float32 [1024], P('fsdp')
- grad_router: float32 [1024], replicated
Inputs may be any that keep to these rules, and one draw needn't show every extreme that they name: `lengths`: each aligned block of 8 entries (one device's sequences, in order) holds multiples of 8 that sum to 4096; exactly one of them equals 2048. `selected`: each aligned block of 512 entries lists distinct positions within its device's 4096 tokens in ascending order; a sequence of length L has exactly L / 8 of its positions listed.
All inputs are finite; a program needn't handle non-finite values.
Results may differ from a plain program's by a relative error of at most 0.014.
Values may be sent and summed in bfloat16 or wider, within the bound.
No kernel may reach another device: no remote copies, remote signals or barrier semaphores. Data moves between devices by JAX's collectives and lax.ppermute only.
A program may use at most 192 MiB of HBM per device.

v0:
```python
import numpy as np
import jax
import jax.numpy as jnp
from jax import lax
from jax.sharding import PartitionSpec as P

HEADS = 16
HEAD = 64
EPS = 1e-06
MASKED = -1e30


def rms_scale(values, gain_vec):
    return values * lax.rsqrt(jnp.mean(values * values, axis=-1, keepdims=True) + EPS) * gain_vec


def seq_mask(lengths, selected):
    seq_ends = jnp.cumsum(lengths)
    owner_seq = jnp.sum((selected[:, None] >= seq_ends[None, :]).astype(jnp.int32), axis=1)
    return (owner_seq[:, None] == owner_seq[None, :]) & (selected[None, :] <= selected[:, None])


def split_heads(matrix):
    return matrix.reshape(matrix.shape[0], HEADS, HEAD)


def masked_scores(query_heads, key_heads, allowed, score_scale):
    scores = (
        jnp.einsum("qhd,khd->hqk", query_heads, key_heads, preferred_element_type=jnp.float32)
        * score_scale
    )
    return jnp.where(allowed[None], scores, MASKED)


def plane_layout(mesh):
    devs = np.asarray(mesh.devices)
    if devs.ndim != 2 or devs.shape[0] != 8:
        return False
    try:
        for j in range(devs.shape[1]):
            for i in range(8):
                here = devs[i, j]
                mate = devs[i ^ 1, j]
                if (
                    tuple(mate.coords) != tuple(here.coords)
                    or mate.core_on_chip == here.core_on_chip
                ):
                    return False
                steps = []
                for bit in (2, 4):
                    other = devs[i ^ bit, j]
                    if other.core_on_chip != here.core_on_chip:
                        return False
                    diff = [abs(a - b) for a, b in zip(other.coords, here.coords)]
                    if sorted(diff) != [0] * (len(diff) - 1) + [1]:
                        return False
                    steps.append(diff.index(1))
                if steps[0] == steps[1]:
                    return False
    except AttributeError:
        return False
    return True


def swap_pairs(bit, size):
    return [(i, i ^ bit) for i in range(size)]


def plane_reduce(grad):
    rows, cols = grad.shape
    part = rows // 8
    half = part // 2
    me = lax.axis_index("fsdp")
    core = me % 2
    xi = me // 2 % 2
    yi = me // 4
    blocks = grad.reshape(4, 2, part, cols)
    keep = lax.dynamic_index_in_dim(blocks, core, axis=1, keepdims=False)
    send = lax.dynamic_index_in_dim(blocks, 1 - core, axis=1, keepdims=False)
    got = lax.ppermute(send.astype(jnp.bfloat16), "fsdp", swap_pairs(1, 8))
    chip = keep + got.astype(jnp.float32)

    def pick(y, x):
        return lax.dynamic_index_in_dim(chip, y * 2 + x, axis=0, keepdims=False)

    own = pick(yi, xi)
    to_x = pick(yi, 1 - xi)
    to_y = pick(1 - yi, xi)
    to_d = pick(1 - yi, 1 - xi)
    first_x = lax.ppermute(
        jnp.stack([to_x[:half], to_d[:half]]).astype(jnp.bfloat16), "fsdp", swap_pairs(2, 8)
    ).astype(jnp.float32)
    first_y = lax.ppermute(
        jnp.stack([to_y[half:], to_d[half:]]).astype(jnp.bfloat16), "fsdp", swap_pairs(4, 8)
    ).astype(jnp.float32)
    own_a = own[:half] + first_x[0]
    pass_a = to_y[:half] + first_x[1]
    own_b = own[half:] + first_y[0]
    pass_b = to_x[half:] + first_y[1]
    second_y = lax.ppermute(pass_a.astype(jnp.bfloat16), "fsdp", swap_pairs(4, 8)).astype(
        jnp.float32
    )
    second_x = lax.ppermute(pass_b.astype(jnp.bfloat16), "fsdp", swap_pairs(2, 8)).astype(
        jnp.float32
    )
    shard = jnp.concatenate([own_a + second_y, own_b + second_x], axis=0)
    return lax.psum(shard.astype(jnp.bfloat16), "dp").astype(jnp.float32)


def plain_reduce(grad):
    shard = lax.psum_scatter(grad.astype(jnp.bfloat16), "fsdp", scatter_dimension=0, tiled=True)
    return lax.psum(shard, "dp").astype(jnp.float32)


def make_per_device(reduce_grad):

    def per_device(
        tokens,
        cotangent,
        lengths,
        selected,
        attn_in,
        attn_out,
        mlp_in,
        mlp_out,
        norm_attn,
        norm_mlp,
        router,
    ):
        model_width = tokens.shape[1]
        row_count = selected.shape[0]
        score_scale = HEAD ** (-0.5)
        w_qkv, gain_attn = (
            lax.all_gather(attn_in, "fsdp", axis=0, tiled=True),
            lax.all_gather(norm_attn, "fsdp", axis=0, tiled=True),
        )
        w_out = lax.all_gather(attn_out, "fsdp", axis=0, tiled=True)
        w_in, gain_mlp = (
            lax.all_gather(mlp_in, "fsdp", axis=0, tiled=True),
            lax.all_gather(norm_mlp, "fsdp", axis=0, tiled=True),
        )
        w_down = lax.all_gather(mlp_out, "fsdp", axis=0, tiled=True)
        gain_one = gain_attn.astype(jnp.float32)
        gain_two = gain_mlp.astype(jnp.float32)
        positions = lax.broadcasted_iota(jnp.int32, (row_count, tokens.shape[0]), 1)
        select = (selected[:, None] == positions).astype(jnp.bfloat16)
        routed = jnp.dot(select, tokens, preferred_element_type=jnp.float32)
        routed_low = routed.astype(jnp.bfloat16)
        router_rate = jnp.dot(routed_low, router, preferred_element_type=jnp.float32)
        allowed = seq_mask(lengths, selected)
        normed_float, norm_pull = jax.vjp(rms_scale, routed, gain_one)
        normed = normed_float.astype(jnp.bfloat16)
        qkv = jnp.dot(normed, w_qkv, preferred_element_type=jnp.float32).astype(jnp.bfloat16)
        query_heads = split_heads(qkv[:, :model_width])
        key_heads = split_heads(qkv[:, model_width : 2 * model_width])
        value_heads = split_heads(qkv[:, 2 * model_width :])
        scores = masked_scores(query_heads, key_heads, allowed, score_scale)
        highest = jnp.max(scores, axis=-1, keepdims=True)
        exponent = jnp.exp(scores - highest)
        row_total = jnp.sum(exponent, axis=-1, keepdims=True)
        probabilities = (exponent / row_total).astype(jnp.bfloat16)
        log_total = highest + jnp.log(row_total)
        attn_mix = jnp.einsum(
            "hqk,khd->qhd", probabilities, value_heads, preferred_element_type=jnp.float32
        )
        attn_mix = attn_mix.reshape(row_count, model_width).astype(jnp.bfloat16)
        attended = jnp.dot(attn_mix, w_out, preferred_element_type=jnp.float32)
        middle = routed + attended
        normed_two_float, middle_pull = jax.vjp(rms_scale, middle, gain_two)
        normed_two = normed_two_float.astype(jnp.bfloat16)
        pre_gelu = jnp.dot(normed_two, w_in, preferred_element_type=jnp.float32)
        active_float, gelu_pull = jax.vjp(jax.nn.gelu, pre_gelu)
        active = active_float.astype(jnp.bfloat16)
        expanded = jnp.dot(active, w_down, preferred_element_type=jnp.float32)
        update = attended + expanded
        branch = (router_rate[:, None] * update).astype(jnp.bfloat16)
        output = (
            tokens.astype(jnp.float32)
            + jnp.einsum("kt,kd->td", select, branch, preferred_element_type=jnp.float32)
        ).astype(jnp.bfloat16)
        cot_rows = jnp.dot(select, cotangent, preferred_element_type=jnp.float32)
        grad_rate = jnp.sum(cot_rows * update, axis=-1)
        grad_update = cot_rows * router_rate[:, None]
        grad_expanded = grad_update.astype(jnp.bfloat16)
        grad_down = jnp.einsum(
            "kf,kd->fd", active, grad_expanded, preferred_element_type=jnp.float32
        )
        shard_down = reduce_grad(grad_down)
        grad_active = jnp.einsum(
            "kd,fd->kf", grad_expanded, w_down, preferred_element_type=jnp.float32
        )
        (grad_inner_float,) = gelu_pull(grad_active)
        grad_inner = grad_inner_float.astype(jnp.bfloat16)
        grad_up = jnp.einsum(
            "kd,kf->df", normed_two, grad_inner, preferred_element_type=jnp.float32
        )
        shard_up = reduce_grad(grad_up)
        grad_normed_two = jnp.einsum(
            "kf,df->kd", grad_inner, w_in, preferred_element_type=jnp.float32
        )
        grad_middle, grad_gain_two = middle_pull(grad_normed_two)
        grad_attended = (grad_update + grad_middle).astype(jnp.bfloat16)
        grad_proj = jnp.einsum(
            "ka,kd->ad", attn_mix, grad_attended, preferred_element_type=jnp.float32
        )
        shard_proj = reduce_grad(grad_proj)
        grad_mix = jnp.einsum(
            "kd,ad->ka", grad_attended, w_out, preferred_element_type=jnp.float32
        ).astype(jnp.bfloat16)
        grad_mix_heads = split_heads(grad_mix)
        scores_again = masked_scores(query_heads, key_heads, allowed, score_scale)
        prob_float = jnp.where(allowed[None], jnp.exp(scores_again - log_total), 0.0)
        grad_probs = jnp.einsum(
            "qhd,khd->hqk", grad_mix_heads, value_heads, preferred_element_type=jnp.float32
        )
        row_delta = jnp.sum(prob_float * grad_probs, axis=-1, keepdims=True)
        grad_scores = (prob_float * (grad_probs - row_delta)).astype(jnp.bfloat16)
        prob_low = prob_float.astype(jnp.bfloat16)
        grad_query = (
            jnp.einsum("hqk,khd->qhd", grad_scores, key_heads, preferred_element_type=jnp.float32)
            * score_scale
        )
        grad_key = (
            jnp.einsum("hqk,qhd->khd", grad_scores, query_heads, preferred_element_type=jnp.float32)
            * score_scale
        )
        grad_value = jnp.einsum(
            "hqk,qhd->khd", prob_low, grad_mix_heads, preferred_element_type=jnp.float32
        )
        grad_qkv = jnp.concatenate(
            [
                grad_query.reshape(row_count, model_width),
                grad_key.reshape(row_count, model_width),
                grad_value.reshape(row_count, model_width),
            ],
            axis=1,
        ).astype(jnp.bfloat16)
        grad_proj_in = jnp.einsum("kd,ke->de", normed, grad_qkv, preferred_element_type=jnp.float32)
        shard_qkv = reduce_grad(grad_proj_in)
        grad_normed = jnp.einsum("ke,de->kd", grad_qkv, w_qkv, preferred_element_type=jnp.float32)
        grad_routed_norm, grad_gain_one = norm_pull(grad_normed)
        grad_routed = (
            grad_routed_norm + grad_middle + grad_rate[:, None] * router.astype(jnp.float32)
        ).astype(jnp.bfloat16)
        grad_tokens = (
            cotangent.astype(jnp.float32)
            + jnp.einsum("kt,kd->td", select, grad_routed, preferred_element_type=jnp.float32)
        ).astype(jnp.bfloat16)
        router_local = jnp.dot(grad_rate, routed, precision=lax.Precision.HIGHEST)
        small = lax.psum(
            jnp.concatenate([grad_gain_one, grad_gain_two, router_local]), ("fsdp", "dp")
        )
        gain_part = grad_gain_one.shape[0] // lax.axis_size("fsdp")
        me = lax.axis_index("fsdp")
        shard_gain_one = lax.dynamic_slice_in_dim(small, me * gain_part, gain_part)
        shard_gain_two = lax.dynamic_slice_in_dim(
            small, grad_gain_one.shape[0] + me * gain_part, gain_part
        )
        grad_router = small[2 * grad_gain_one.shape[0] :]
        return (
            output,
            grad_tokens,
            shard_qkv,
            shard_proj,
            shard_up,
            shard_down,
            shard_gain_one,
            shard_gain_two,
            grad_router,
        )

    return per_device


def solution(mesh):
    placed = (
        P(("fsdp", "dp"), None),
        P(("fsdp", "dp"), None),
        P(("fsdp", "dp")),
        P(("fsdp", "dp")),
        P("fsdp", None),
        P("fsdp", None),
        P("fsdp", None),
        P("fsdp", None),
        P("fsdp"),
        P("fsdp"),
        P(),
    )
    reduce_grad = plane_reduce if plane_layout(mesh) else plain_reduce
    return jax.shard_map(
        make_per_device(reduce_grad),
        mesh=mesh,
        in_specs=placed,
        out_specs=(
            P(("fsdp", "dp"), None),
            P(("fsdp", "dp"), None),
            P("fsdp", None),
            P("fsdp", None),
            P("fsdp", None),
            P("fsdp", None),
            P("fsdp"),
            P("fsdp"),
            P(),
        ),
        check_vma=False,
    )
```

profile of v0, /device:TPU:0, one launch (start us, length us, event | category | flops | bytes accessed | tf_op | source)
XLA Modules:
  0.0 639.2 jit_solution(1268586833503978225)
XLA Ops:
  12.9 10.4 %all-gather = bf16[8,1,128]{2,1,0:T(2,128)(2,1)S(1)} all-gather(bf16[1,1,128]{2,1,0:T(2,128)(2,1)} %bitcast.194), channel_id=1, replica_groups=mesh['fsdp'=8,'dp'=4] {'fsdp'}, dimensions={0}, use_global_device_ids=true | all-gather | bytes 2304 | tf_op jit(solution)/shard_map/all_gather | solution.py:135
  23.3 8.8 %all-gather.1 = bf16[8,1,128]{2,1,0:T(2,128)(2,1)S(1)} all-gather(bf16[1,1,128]{2,1,0:T(2,128)(2,1)} %bitcast.195), channel_id=1, replica_groups=mesh['fsdp'=8,'dp'=4] {'fsdp'}, dimensions={0}, use_global_device_ids=true | all-gather | bytes 2304 | tf_op jit(solution)/shard_map/all_gather | solution.py:140
  32.9 7.8 %multiply_reduce_fusion.7 = (f32[512]{0:T(512)S(1)}, f32[512,1024]{1,0:T(8,128)S(1)}) fusion(bf16[4096,1024]{1,0:T(8,128)(2,1)} %param.11, s32[512]{0:T(512)} %param.14), kind=kOutput, calls=%fused_computation.64 | convolution fusion | flops 4298112512 | bytes 10489856 | tf_op jit(solution)/shard_map/dot_general | solution.py:147
  41.4 9.3 %fusion.12 = f32[512,1024]{1,0:T(8,128)} fusion(bf16[4096,1024]{1,0:T(8,128)(2,1)} %param.12, s32[512]{0:T(512)S(1)} %copy-done.15), kind=kOutput, calls=%fused_computation.28 | convolution fusion | flops 4297064448 | bytes 10487808 | tf_op jit(solution)/shard_map/dot_general | solution.py:181
  50.7 7.4 %all-gather.7.cloned.1.call-done = bf16[1024,3072]{1,0:T(8,128)(2,1)} async-done(((bf16[128,3072]{1,0:T(8,128)(2,1)}), bf16[1024,3072]{1,0:T(8,128)(2,1)}) %all-gather.7.cloned.1.call-update) | async-done | bytes 6291472 | tf_op jit(solution)/shard_map/all_gather | solution.py:134
  58.0 6.6 %convolution_convert_fusion = bf16[512,3072]{1,0:T(8,128)(2,1)S(1)} fusion(bf16[1024,3072]{1,0:T(8,128)(2,1)} %all-gather.7.cloned.1.call-done, f32[512,1024]{1,0:T(8,128)S(1)} %get-tuple-element.59, f32[1024]{0:T(1024)S(1)} %bitcast.180, f32[512]{0:T(512)S(1)} %fusion.84), kind=kOutput, calls=%fused_computation.34 | convolution fusion | flops 3224371200 | bytes 11540480 | tf_op jit(solution)/shard_map/dot_general | solution.py:153
  64.6 1.7 fusion.97
  66.4 1.5 copy.59
  67.9 2.3 copy.58
  70.2 2.3 copy.57
  72.4 8.8 %fusion.1 = (f32[16,512]{1,0:T(8,128)S(1)}, f32[16,512,512]{1,2,0:T(8,128)}) fusion(pred[512,512]{0,1:T(8,128)(4,1)S(1)} %compare_and_fusion, bf16[512,16,64]{0,2,1:T(8,128)(2,1)} %bitcast.161, bf16[512,16,64]{0,2,1:T(8,128)(2,1)S(1)} %bitcast.159), kind=kOutput, calls=%fused_computation.11 | convolution fusion | flops 549445632 | bytes 19169280 | tf_op jit(solution)/shard_map/qhd,khd->hqk/dot_general | solution.py:29
  81.3 9.3 %fusion = f32[16,512]{1,0:T(8,128)S(1)} fusion(f32[16,512,512]{1,2,0:T(8,128)} %get-tuple-element.61, f32[16,512]{1,0:T(8,128)S(1)} %get-tuple-element.60, pred[512,512]{0,1:T(8,128)(4,1)S(1)} %compare_and_fusion), kind=kLoop, calls=%fused_computation.8 | loop fusion | flops 16769024 | bytes 17104896 | tf_op jit(solution)/shard_map/reduce_sum | solution.py:160
  90.6 9.5 %fusion.26 = bf16[16,64,512]{2,1,0:T(8,128)(2,1)} fusion(bf16[512,16,64]{0,2,1:T(8,128)(2,1)} %bitcast.175, f32[16,512,512]{1,2,0:T(8,128)} %get-tuple-element.61, f32[16,512]{1,0:T(8,128)S(1)} %fusion, f32[16,512]{1,0:T(8,128)S(1)} %get-tuple-element.60, pred[512,512]{0,1:T(8,128)(4,1)S(1)} %compare_and_fusion), kind=kOutput, calls=%fused_computation.68 | convolution fusion | flops 558366720 | bytes 19202048 | tf_op jit(solution)/shard_map/hqk,khd->qhd/dot_general | solution.py:163
  100.1 5.2 multiply_reduce_fusion.6
  105.3 38.6 %all-gather.11.cloned.1.call-done = bf16[1024,4096]{1,0:T(8,128)(2,1)} async-done(((bf16[128,4096]{1,0:T(8,128)(2,1)}), bf16[1024,4096]{1,0:T(8,128)(2,1)}) %all-gather.11.cloned.1.call-update) | async-done | bytes 8388624 | tf_op jit(solution)/shard_map/all_gather | solution.py:139
  143.9 7.8 %fusion.96 = f32[512,4096]{1,0:T(8,128)S(1)} fusion(bf16[1024,4096]{1,0:T(8,128)(2,1)} %all-gather.11.cloned.1.call-done, f32[512,1024]{1,0:T(8,128)} %get-tuple-element.18, f32[1024]{0:T(1024)S(1)} %bitcast.184, f32[512]{0:T(512)S(1)} %fusion.85), kind=kOutput, calls=%fused_computation.181 | convolution fusion | flops 4296540160 | bytes 18880512 | tf_op jit(solution)/shard_map/dot_general | solution.py:171
  151.7 3.7 copy-done.39
  155.4 9.2 %fusion.93 = f32[4096,1024]{1,0:T(8,128)} fusion(f32[512,1024]{1,0:T(8,128)S(1)} %copy-done.40, f32[512]{0:T(512)S(1)} %bitcast.189, f32[512,4096]{1,0:T(8,128)S(1)} %fusion.96), kind=kOutput, calls=%fused_computation.178 | convolution fusion | flops 4314890240 | bytes 27265024 | tf_op jit(solution)/shard_map/kf,kd->fd/dot_general | solution.py:185
  164.7 35.3 %all-gather.13.cloned.1.call-done = bf16[4096,1024]{1,0:T(8,128)(2,1)} async-done(((bf16[512,1024]{1,0:T(8,128)(2,1)}), bf16[4096,1024]{1,0:T(8,128)(2,1)}) %all-gather.13.cloned.1.call-update) | async-done | bytes 8388624 | tf_op jit(solution)/shard_map/all_gather | solution.py:142
  199.9 13.3 %fusion.8 = bf16[512,4096]{1,0:T(8,128)(2,1)S(1)} fusion(f32[512,4096]{1,0:T(8,128)} %copy-done.39, bf16[4096,1024]{1,0:T(8,128)(2,1)} %all-gather.13.cloned.1.call-done, f32[512,1024]{1,0:T(8,128)} %fusion.12, f32[512]{0:T(512)S(1)} %bitcast.190), kind=kOutput, calls=%fused_computation.18 | convolution fusion | flops 4337958912 | bytes 23070720 | tf_op jit(solution)/shard_map/kd,fd->kf/dot_general | solution.py:189
  213.3 2.0 copy-done.38
  215.3 8.4 %fusion.95 = f32[1024,4096]{1,0:T(8,128)} fusion(bf16[512,4096]{1,0:T(8,128)(2,1)S(1)} %fusion.8, f32[512,1024]{1,0:T(8,128)S(1)} %copy-done.4, f32[1024]{0:T(1024)S(1)} %bitcast.185, f32[512]{0:T(512)S(1)} %fusion.85), kind=kOutput, calls=%fused_computation.180 | convolution fusion | flops 4296540160 | bytes 23074816 | tf_op jit(solution)/shard_map/kd,kf->df/dot_general | solution.py:194
  223.7 11.5 %multiply_reduce_fusion.1 = (f32[1024]{0:T(1024)}, f32[512]{0:T(512)S(1)}, f32[512,1024]{1,0:T(8,128)}) fusion(f32[512,1024]{1,0:T(8,128)S(1)} %copy-done.4, f32[512]{0:T(512)S(1)} %fusion.85, f32[1024]{0:T(1024)S(1)} %bitcast.186, bf16[512,4096]{1,0:T(8,128)(2,1)} %copy-done.38, bf16[1024,4096]{1,0:T(8,128)(2,1)} %all-gather.11.cloned.1.call-done), kind=kOutput, calls=%fused_computation.49 | convolution fusion | flops 4298111488 | bytes 16789504 | tf_op jit(solution)/shard_map/kf,df->kd/dot_general | solution.py:198
  235.3 10.3 %multiply_reduce_fusion.3 = (f32[512]{0:T(512)S(1)}, bf16[512,1024]{1,0:T(8,128)(2,1)S(1)}, f32[512,1024]{1,0:T(8,128)}) fusion(f32[512,1024]{1,0:T(8,128)S(1)} %copy-done.41, f32[512,1024]{1,0:T(8,128)S(1)} %copy-done.4, f32[512]{0:T(512)S(1)} %multiply_multiply_fusion.3, f32[512]{0:T(512)S(1)} %fusion.85, f32[512,1024]{1,0:T(8,128)} %get-tuple-element.63, ...), kind=kOutput, calls=%fused_computation.54 | convolution fusion | flops 4319608320 | bytes 28323840 | tf_op jit(solution)/shard_map/dot_general | solution.py:174
  246.7 2.3 convolution_convert_fusion.1
  248.9 2.3 copy.61
  251.2 11.5 %fusion.27 = bf16[16,64,512]{2,1,0:T(8,128)(2,1)} fusion(bf16[512,16,64]{0,2,1:T(8,128)(2,1)} %bitcast.177, f32[16,512]{1,0:T(8,128)S(1)} %log_add_fusion, f32[16,512,512]{1,2,0:T(8,128)} %get-tuple-element.61, pred[512,512]{0,1:T(8,128)(4,1)S(1)} %compare_and_fusion), kind=kOutput, calls=%fused_computation.70 | convolution fusion | flops 558366720 | bytes 19169280 | tf_op jit(solution)/shard_map/hqk,qhd->khd/dot_general | solution.py:227
  262.8 12.5 %multiply_reduce_fusion = (f32[16,512]{1,0:T(8,128)S(1)}, f32[16,512,512]{1,2,0:T(8,128)}) fusion(f32[16,512]{1,0:T(8,128)S(1)} %log_add_fusion, f32[16,512,512]{1,2,0:T(8,128)} %get-tuple-element.61, pred[512,512]{0,1:T(8,128)(4,1)S(1)} %compare_and_fusion, bf16[512,16,64]{0,2,1:T(8,128)(2,1)S(1)} %bitcast.178, bf16[512,16,64]{0,2,1:T(8,128)(2,1)S(1)} %bitcast.176), kind=kOutput, calls=%fused_computation.2 | convolution fusion | flops 562028544 | bytes 35979264 | tf_op jit(solution)/shard_map/qhd,khd->hqk/dot_general | solution.py:213
  275.2 12.6 %multiply_convert_fusion = bf16[16,512,512]{1,2,0:T(8,128)(2,1)S(1)} fusion(f32[16,512,512]{1,2,0:T(8,128)} %get-tuple-element.66, f32[16,512]{1,0:T(8,128)S(1)} %get-tuple-element.65, f32[16,512]{1,0:T(8,128)S(1)} %log_add_fusion, f32[16,512,512]{1,2,0:T(8,128)} %get-tuple-element.61, pred[512,512]{0,1:T(8,128)(4,1)S(1)} %compare_and_fusion), kind=kLoop, calls=%fused_computation.1 | loop fusion | flops 29360128 | bytes 42270720 | tf_op jit(solution)/shard_map/convert_element_type | solution.py:217
  287.8 2.6 multiply_convert_fusion.2
  290.5 1.5 multiply_convert_fusion.3
  293.8 6.0 fusion.17
  300.0 4.9 fusion.30
  305.0 2.1 fusion.22
  307.4 6.0 fusion.16
  313.7 9.0 %multiply_reduce_fusion.2 = (f32[1024]{0:T(1024)}, f32[512]{0:T(512)S(1)}, f32[512,1024]{1,0:T(8,128)}) fusion(f32[512,1024]{1,0:T(8,128)S(1)} %get-tuple-element.59, f32[512]{0:T(512)S(1)} %copy-done.34, f32[1024]{0:T(1024)S(1)} %bitcast.182, bf16[1024,3072]{1,0:T(8,128)(2,1)} %all-gather.7.cloned.1.call-done, bf16[512,1024]{0,1:T(8,128)(2,1)} %bitcast.201, ...), kind=kOutput, calls=%fused_computation.50 | convolution fusion | flops 3233806848 | bytes 13643776 | tf_op jit(solution)/shard_map/ke,de->kd/dot_general | solution.py:240
  322.7 1.6 bitcast_add_fusion.3
  327.7 5.3 collective-permute-done.8
  335.0 2.9 bitcast_add_fusion.2
  338.1 2.5 copy-done
  346.4 52.0 %psum.39 = f32[3072]{0:T(1024)} all-reduce(f32[3072]{0:T(1024)S(1)} %pad_maximum_fusion.15), channel_id=1, replica_groups=mesh['fsdp'=8,'dp'=4] {'fsdp','dp'}, use_global_device_ids=true, to_apply=%region_16.17 | all-reduce | flops 3072 | bytes 24576 | tf_op jit(solution)/shard_map/psum | solution.py:250
  398.5 1.3 slice.283
  399.8 1.3 fusion.102
  405.5 2.4 fusion.72
  408.0 2.7 collective-permute-start.2
  411.9 5.8 bitcast_add_fusion.1
  419.7 10.3 %bitcast_add_fusion = f32[4,512,1024]{2,1,0:T(8,128)} fusion(bf16[4,512,1024]{2,1,0:T(8,128)(2,1)} %collective-permute-done.15, f32[4,2,512,1024]{3,2,1,0:T(8,128)} %bitcast.164, s32[]{:T(128)S(6)} %select_n.97), kind=kLoop, calls=%fused_computation.21 | loop fusion | flops 4194304 | bytes 20971524 | tf_op jit(solution)/shard_map/add | solution.py:81
  429.9 1.9 dynamic-slice_convert_fusion
  431.9 1.7 dynamic-slice_convert_fusion.5
  435.0 2.1 collective-permute-start.13
  438.5 1.7 fusion.67
  440.2 19.6 %collective-permute-done.18 = bf16[2,256,1024]{2,1,0:T(8,128)(2,1)S(1)} collective-permute-done((bf16[2,256,1024]{2,1,0:T(8,128)(2,1)S(1)}, bf16[2,256,1024]{2,1,0:T(8,128)(2,1)S(1)}, u32[]{:S(2)}, u32[]{:S(2)}) %collective-permute-start.18) | collective-permute-done | bytes 1048608 | tf_op jit(solution)/shard_map/ppermute | solution.py:93
  460.9 1.7 collective-permute-start.17
  463.5 18.8 %collective-permute-done.13 = bf16[2,64,4096]{2,1,0:T(8,128)(2,1)S(1)} collective-permute-done((bf16[2,64,4096]{2,1,0:T(8,128)(2,1)S(1)}, bf16[2,64,4096]{2,1,0:T(8,128)(2,1)S(1)}, u32[]{:S(2)}, u32[]{:S(2)}) %collective-permute-start.13) | collective-permute-done | bytes 1048608 | tf_op jit(solution)/shard_map/ppermute | solution.py:93
  483.3 1.7 collective-permute-start.12
  486.8 6.7 %collective-permute-done.17 = bf16[256,1024]{1,0:T(8,128)(2,1)S(1)} collective-permute-done((bf16[256,1024]{1,0:T(8,128)(2,1)S(1)}, bf16[256,1024]{1,0:T(8,128)(2,1)S(1)}, u32[]{:S(2)}, u32[]{:S(2)}) %collective-permute-start.17) | collective-permute-done | bytes 524320 | tf_op jit(solution)/shard_map/ppermute | solution.py:100
  495.8 5.9 collective-permute-done.12
  504.3 10.0 %add_convert_fusion.1 = bf16[4096,1024]{1,0:T(8,128)(2,1)} fusion(bf16[4096,1024]{1,0:T(8,128)(2,1)} %param.11, s32[512]{0:T(512)S(1)} %copy-done.16, f32[512,1024]{1,0:T(8,128)} %get-tuple-element.64, f32[512]{0:T(512)S(1)} %bitcast.192), kind=kOutput, calls=%fused_computation.4 | convolution fusion | flops 4310695936 | bytes 18878464 | tf_op jit(solution)/shard_map/kt,kd->td/dot_general | solution.py:179
  514.4 11.7 %add_convert_fusion = bf16[4096,1024]{1,0:T(8,128)(2,1)} fusion(bf16[4096,1024]{1,0:T(8,128)(2,1)} %param.12, s32[512]{0:T(512)S(1)} %copy-done.16, f32[512,1024]{1,0:T(8,128)S(1)} %get-tuple-element.59, f32[512,1024]{1,0:T(8,128)S(1)} %copy-done.42, f32[1024]{0:T(1024)S(1)} %copy-done.19, f32[512]{0:T(512)S(1)} %copy-done.29, f32[512]{0:T(512)S(1)} %copy-done.32, ...), kind=kOutput, calls=%fused_computation | convolution fusion | flops 4316987392 | bytes 25190400 | tf_op jit(solution)/shard_map/kt,kd->td/dot_general | solution.py:247
  526.0 97.5 %all-reduce.3.cloned.1.call-done = (bf16[128,3072]{1,0:T(8,128)(2,1)}, bf16[128,1024]{1,0:T(8,128)(2,1)}, bf16[128,4096]{1,0:T(8,128)(2,1)}, bf16[512,1024]{1,0:T(8,128)(2,1)}) async-done(((bf16[128,3072]{1,0:T(8,128)(2,1)}, bf16[128,1024]{1,0:T(8,128)(2,1)}, bf16[128,4096]{1,0:T(8,128)(2,1)}, bf16[512,1024]{1,0:T(8,128)(2,1)}), (bf16[128,3072]{1,0:T(8,128)(2,1)}, bf16[128,1024]{1,0:T(8,128)(2,1)}, ...) | async-done | bytes 3145744 | tf_op jit(solution)/shard_map/psum | solution.py:107
  623.6 1.9 convert_element_type.281
  625.4 2.4 convert_element_type.269
  627.9 2.8 convert_element_type.293
  630.6 1.6 convert_element_type.305
  (190 shorter events, 42.0 us)
Async XLA Ops:
  7.2 50.9 %all-gather.7.cloned.1.call-start = ((), (), s32[]{:S(2)}) async-start(), calls=%async_computation | async-start | bytes 7077888 | tf_op jit(solution)/shard_map/all_gather | solution.py:134
  7.9 92.2 %all-gather.9.cloned.1.call-start = ((), (), s32[]{:S(2)}) async-start(), calls=%async_computation.1 | async-start | bytes 2359296 | tf_op jit(solution)/shard_map/all_gather | solution.py:137
  8.7 135.2 %all-gather.11.cloned.1.call-start = ((), (), s32[]{:S(2)}) async-start(), calls=%async_computation.2 | async-start | bytes 9437184 | tf_op jit(solution)/shard_map/all_gather | solution.py:139
  9.4 190.5 %all-gather.13.cloned.1.call-start = ((), (), s32[]{:S(2)}) async-start(), calls=%async_computation.3 | async-start | bytes 9437184 | tf_op jit(solution)/shard_map/all_gather | solution.py:142
  10.0 613.6 %all-reduce.3.cloned.1.call-start = ((), (), s32[]{:S(2)}) async-start(), calls=%async_computation.4 | async-start | bytes 6291456 | tf_op jit(solution)/shard_map/psum | solution.py:107
  23.3 34.8 %copy-start.20 = (f32[8,1,128]{2,1,0:T(1,128)}, f32[8,1,128]{2,1,0:T(1,128)S(1)}, u32[]{:S(2)}) copy-start(f32[8,1,128]{2,1,0:T(1,128)S(1)} %convert_element_type.306) | copy-start | bytes 12292
  32.1 203.1 %copy-start.22 = (f32[8,1,128]{2,1,0:T(1,128)}, f32[8,1,128]{2,1,0:T(1,128)S(1)}, u32[]{:S(2)}) copy-start(f32[8,1,128]{2,1,0:T(1,128)S(1)} %convert_element_type.307) | copy-start | bytes 12292
  32.9 7.8 %copy-start.15 = (s32[512]{0:T(512)S(1)}, s32[512]{0:T(512)}, u32[]{:S(2)}) copy-start(s32[512]{0:T(512)} %param.14) | copy-start | bytes 6148
  40.7 17.3 %copy-start.33 = (f32[512]{0:T(512)}, f32[512]{0:T(512)S(1)}, u32[]{:S(2)}) copy-start(f32[512]{0:T(512)S(1)} %fusion.84) | copy-start | bytes 6148
  41.4 193.8 %copy-start.26 = (f32[1,512]{1,0:T(1,128)}, f32[1,512]{1,0:T(1,128)S(1)}, u32[]{:S(2)}) copy-start(f32[1,512]{1,0:T(1,128)S(1)} %fusion.58) | copy-start | bytes 6148
  105.3 129.9 %copy-start.36 = (f32[512]{0:T(512)}, f32[512]{0:T(512)S(1)}, u32[]{:S(2)}) copy-start(f32[512]{0:T(512)S(1)} %fusion.85) | copy-start | bytes 6148
  143.9 11.5 %copy-start.40 = (f32[512,1024]{1,0:T(8,128)S(1)}, f32[512,1024]{1,0:T(8,128)}, u32[]{:S(2)}) copy-start(f32[512,1024]{1,0:T(8,128)} %fusion.12) | copy-start | bytes 6291460
  199.9 15.4 %copy-start.4 = (f32[512,1024]{1,0:T(8,128)S(1)}, f32[512,1024]{1,0:T(8,128)}, u32[]{:S(2)}) copy-start(f32[512,1024]{1,0:T(8,128)} %get-tuple-element.18) | copy-start | bytes 6291460
  215.3 19.9 %slice-start.2 = ((s8[8388608]{0:T(1024)(128)(4,1)}), s8[4194304]{0:T(1024)(128)(4,1)S(1)}, s32[]{:S(2)}) async-start(s8[8388608]{0:T(1024)(128)(4,1)} %bitcast.197), calls=%async_computation.7 | async-start | bytes 8388608
  223.7 11.6 %copy-start.6 = (f32[512,1024]{1,0:T(8,128)S(1)}, f32[512,1024]{1,0:T(8,128)}, u32[]{:S(2)}) copy-start(f32[512,1024]{1,0:T(8,128)} %get-tuple-element.62) | copy-start | bytes 6291460
  223.7 11.6 %slice-start.3 = ((s8[8388608]{0:T(1024)(128)(4,1)}), s8[4194304]{0:T(1024)(128)(4,1)S(1)}, s32[]{:S(2)}) async-start(s8[8388608]{0:T(1024)(128)(4,1)} %bitcast.197), calls=%async_computation.8 | async-start | bytes 8388608
  223.7 11.6 %copy-start.41 = (f32[512,1024]{1,0:T(8,128)S(1)}, f32[512,1024]{1,0:T(8,128)}, u32[]{:S(2)}) copy-start(f32[512,1024]{1,0:T(8,128)} %fusion.12) | copy-start | bytes 6291460
  235.2 10.4 %copy-start.30 = (f32[512]{0:T(512)}, f32[512]{0:T(512)S(1)}, u32[]{:S(2)}) copy-start(f32[512]{0:T(512)S(1)} %multiply_multiply_fusion.3) | copy-start | bytes 6148
  235.3 11.4 %copy-start.8 = (bf16[1024,1024]{1,0:T(8,128)(2,1)S(1)}, bf16[1024,1024]{1,0:T(8,128)(2,1)}, u32[]{:S(2)}) copy-start(bf16[1024,1024]{1,0:T(8,128)(2,1)} %all-gather.9.cloned.1.call-done) | copy-start | bytes 6291460
  245.6 80.9 %copy-start.28 = (f32[512]{0:T(512)}, f32[512]{0:T(512)S(1)}, u32[]{:S(2)}) copy-start(f32[512]{0:T(512)S(1)} %get-tuple-element.46) | copy-start | bytes 6148
  251.2 11.6 %copy-start.11 = (bf16[512,1024]{0,1:T(8,128)(2,1)S(1)}, bf16[512,1024]{0,1:T(8,128)(2,1)}, u32[]{:S(2)}) copy-start(bf16[512,1024]{0,1:T(8,128)(2,1)} %copy.57) | copy-start | bytes 3145732
  251.2 11.6 %copy-start.12 = (bf16[512,1024]{0,1:T(8,128)(2,1)S(1)}, bf16[512,1024]{0,1:T(8,128)(2,1)}, u32[]{:S(2)}) copy-start(bf16[512,1024]{0,1:T(8,128)(2,1)} %copy.61) | copy-start | bytes 3145732
  275.2 12.6 %copy-start.1 = (bf16[512,1024]{0,1:T(8,128)(2,1)S(1)}, bf16[512,1024]{0,1:T(8,128)(2,1)}, u32[]{:S(2)}) copy-start(bf16[512,1024]{0,1:T(8,128)(2,1)} %copy.58) | copy-start | bytes 3145732
  293.2 6.8 %copy-start.21 = (f32[8,1,128]{2,1,0:T(1,128)S(1)}, f32[8,1,128]{2,1,0:T(1,128)}, u32[]{:S(2)}) copy-start(f32[8,1,128]{2,1,0:T(1,128)} %copy-done.20) | copy-start | bytes 12292
  293.3 6.8 %copy-start.34 = (f32[512]{0:T(512)S(1)}, f32[512]{0:T(512)}, u32[]{:S(2)}) copy-start(f32[512]{0:T(512)} %copy-done.33) | copy-start | bytes 6148
  293.4 29.2 %collective-permute-start.5 = (bf16[4,128,1024]{2,1,0:T(8,128)(2,1)S(1)}, bf16[4,128,1024]{2,1,0:T(8,128)(2,1)}, u32[]{:S(2)}, u32[]{:S(2)}) collective-permute-start(bf16[4,128,1024]{2,1,0:T(8,128)(2,1)S(1)} %fusion.32), channel_id=1, source_target_pairs={{0,4},{4,0},{8,12},{12,8},{16,20},{20,16},{24,28},{28,24},{1,5},{5... | collective-permute-start | bytes 3145736 | tf_op jit(solution)/shard_map/ppermute | solution.py:80
  299.8 119.9 %collective-permute-start.15 = (bf16[4,512,1024]{2,1,0:T(8,128)(2,1)}, bf16[4,512,1024]{2,1,0:T(8,128)(2,1)}, u32[]{:S(2)}, u32[]{:S(2)}) collective-permute-start(bf16[4,512,1024]{2,1,0:T(8,128)(2,1)} %fusion.17), channel_id=1, source_target_pairs={{0,4},{4,0},{8,12},{12,8},{16,20},{20,16},{24,28},{28,24},{1,5},{5... | collective-permute-start | bytes 12582920 | tf_op jit(solution)/shard_map/ppermute | solution.py:80
  307.1 27.8 %collective-permute-start = (bf16[4,128,3072]{2,1,0:T(8,128)(2,1)}, bf16[4,128,3072]{2,1,0:T(8,128)(2,1)}, u32[]{:S(2)}, u32[]{:S(2)}) collective-permute-start(bf16[4,128,3072]{2,1,0:T(8,128)(2,1)} %fusion.22), channel_id=1, source_target_pairs={{0,4},{4,0},{8,12},{12,8},{16,20},{20,16},{24,28},{28,24},{1,5},{5... | collective-permute-start | bytes 9437192 | tf_op jit(solution)/shard_map/ppermute | solution.py:80
  313.4 98.5 %collective-permute-start.10 = (bf16[4,128,4096]{2,1,0:T(8,128)(2,1)}, bf16[4,128,4096]{2,1,0:T(8,128)(2,1)}, u32[]{:S(2)}, u32[]{:S(2)}) collective-permute-start(bf16[4,128,4096]{2,1,0:T(8,128)(2,1)} %fusion.16), channel_id=1, source_target_pairs={{0,4},{4,0},{8,12},{12,8},{16,20},{20,16},{24,28},{28,24},{1,5},{5... | collective-permute-start | bytes 12582920 | tf_op jit(solution)/shard_map/ppermute | solution.py:80
  324.2 10.7 %copy-start.3 = (f32[4,128,1024]{2,1,0:T(8,128)}, f32[4,128,1024]{2,1,0:T(8,128)S(1)}, u32[]{:S(2)}) copy-start(f32[4,128,1024]{2,1,0:T(8,128)S(1)} %bitcast_add_fusion.3) | copy-start | bytes 6291460
  324.4 8.5 %collective-permute-start.8 = (bf16[2,64,1024]{2,1,0:T(8,128)(2,1)S(1)}, bf16[2,64,1024]{2,1,0:T(8,128)(2,1)S(1)}, u32[]{:S(2)}, u32[]{:S(2)}) collective-permute-start(bf16[2,64,1024]{2,1,0:T(8,128)(2,1)S(1)} %pad_maximum_fusion.13), channel_id=1, source_target_pairs={{0,16},{4,20},{8,24},{12,28},{16,0},{20,4},{24,8},{28,12},{1,17},{... | collective-permute-start | bytes 786440 | tf_op jit(solution)/shard_map/ppermute | solution.py:93
  325.6 8.2 %collective-permute-start.6 = (bf16[2,64,1024]{2,1,0:T(8,128)(2,1)S(1)}, bf16[2,64,1024]{2,1,0:T(8,128)(2,1)S(1)}, u32[]{:S(2)}, u32[]{:S(2)}) collective-permute-start(bf16[2,64,1024]{2,1,0:T(8,128)(2,1)S(1)} %pad_maximum_fusion.12), channel_id=1, source_target_pairs={{0,8},{4,12},{8,0},{12,4},{16,24},{20,28},{24,16},{28,20},{1,9},{5... | collective-permute-start | bytes 786440 | tf_op jit(solution)/shard_map/ppermute | solution.py:90
  334.0 11.3 %collective-permute-start.7 = (bf16[64,1024]{1,0:T(8,128)(2,1)S(1)}, bf16[64,1024]{1,0:T(8,128)(2,1)S(1)}, u32[]{:S(2)}, u32[]{:S(2)}) collective-permute-start(bf16[64,1024]{1,0:T(8,128)(2,1)S(1)} %get-tuple-element.42), channel_id=1, source_target_pairs={{0,16},{4,20},{8,24},{12,28},{16,0},{20,4},{24,8},{28,12},{1,17},{... | collective-permute-start | bytes 393224 | tf_op jit(solution)/shard_map/ppermute | solution.py:100
  337.9 6.8 %copy-start.18 = (f32[512]{0:T(512)S(1)}, f32[512]{0:T(512)}, u32[]{:S(2)}) copy-start(f32[512]{0:T(512)} %copy-done.17) | copy-start | bytes 6148
  337.9 8.5 %copy-start.24 = (f32[1024]{0:T(1024)S(1)}, f32[1024]{0:T(1024)}, u32[]{:S(2)}) copy-start(f32[1024]{0:T(1024)} %get-tuple-element.11) | copy-start | bytes 12292
  337.9 8.5 %copy-start.25 = (f32[1024]{0:T(1024)S(1)}, f32[1024]{0:T(1024)}, u32[]{:S(2)}) copy-start(f32[1024]{0:T(1024)} %get-tuple-element.9) | copy-start | bytes 12292
  341.7 61.2 %collective-permute-start.3 = (bf16[2,64,3072]{2,1,0:T(8,128)(2,1)}, bf16[2,64,3072]{2,1,0:T(8,128)(2,1)}, u32[]{:S(2)}, u32[]{:S(2)}) collective-permute-start(bf16[2,64,3072]{2,1,0:T(8,128)(2,1)} %pad_maximum_fusion.10), channel_id=1, source_target_pairs={{0,16},{4,20},{8,24},{12,28},{16,0},{20,4},{24,8},{28,12},{1,17},{... | collective-permute-start | bytes 2359304 | tf_op jit(solution)/shard_map/ppermute | solution.py:93
  343.8 60.4 %collective-permute-start.1 = (bf16[2,64,3072]{2,1,0:T(8,128)(2,1)}, bf16[2,64,3072]{2,1,0:T(8,128)(2,1)}, u32[]{:S(2)}, u32[]{:S(2)}) collective-permute-start(bf16[2,64,3072]{2,1,0:T(8,128)(2,1)} %pad_maximum_fusion.9), channel_id=1, source_target_pairs={{0,8},{4,12},{8,0},{12,4},{16,24},{20,28},{24,16},{28,20},{1,9},{5... | collective-permute-start | bytes 2359304 | tf_op jit(solution)/shard_map/ppermute | solution.py:90
  345.3 55.7 %collective-permute-start.9 = (bf16[64,1024]{1,0:T(8,128)(2,1)S(1)}, bf16[64,1024]{1,0:T(8,128)(2,1)S(1)}, u32[]{:S(2)}, u32[]{:S(2)}) collective-permute-start(bf16[64,1024]{1,0:T(8,128)(2,1)S(1)} %get-tuple-element.43), channel_id=1, source_target_pairs={{0,8},{4,12},{8,0},{12,4},{16,24},{20,28},{24,16},{28,20},{1,9},{5... | collective-permute-start | bytes 393224 | tf_op jit(solution)/shard_map/ppermute | solution.py:103
  408.0 29.2 %collective-permute-start.2 = (bf16[64,3072]{1,0:T(8,128)(2,1)}, bf16[64,3072]{1,0:T(8,128)(2,1)S(1)}, u32[]{:S(2)}, u32[]{:S(2)}) collective-permute-start(bf16[64,3072]{1,0:T(8,128)(2,1)} %get-tuple-element.33), channel_id=1, source_target_pairs={{0,16},{4,20},{8,24},{12,28},{16,0},{20,4},{24,8},{28,12},{1,17},{... | collective-permute-start | bytes 1179656 | tf_op jit(solution)/shard_map/ppermute | solution.py:100
  410.7 27.8 %collective-permute-start.4 = (bf16[64,3072]{1,0:T(8,128)(2,1)}, bf16[64,3072]{1,0:T(8,128)(2,1)}, u32[]{:S(2)}, u32[]{:S(2)}) collective-permute-start(bf16[64,3072]{1,0:T(8,128)(2,1)} %get-tuple-element.34), channel_id=1, source_target_pairs={{0,8},{4,12},{8,0},{12,4},{16,24},{20,28},{24,16},{28,20},{1,9},{5... | collective-permute-start | bytes 1179656 | tf_op jit(solution)/shard_map/ppermute | solution.py:103
  433.7 26.1 %collective-permute-start.18 = (bf16[2,256,1024]{2,1,0:T(8,128)(2,1)S(1)}, bf16[2,256,1024]{2,1,0:T(8,128)(2,1)S(1)}, u32[]{:S(2)}, u32[]{:S(2)}) collective-permute-start(bf16[2,256,1024]{2,1,0:T(8,128)(2,1)S(1)} %pad_maximum_fusion.7), channel_id=1, source_target_pairs={{0,16},{4,20},{8,24},{12,28},{16,0},{20,4},{24,8},{28,12},{1,17},{... | collective-permute-start | bytes 3145736 | tf_op jit(solution)/shard_map/ppermute | solution.py:93
  434.3 26.1 %collective-permute-start.16 = (bf16[2,256,1024]{2,1,0:T(8,128)(2,1)S(1)}, bf16[2,256,1024]{2,1,0:T(8,128)(2,1)S(1)}, u32[]{:S(2)}, u32[]{:S(2)}) collective-permute-start(bf16[2,256,1024]{2,1,0:T(8,128)(2,1)S(1)} %pad_maximum_fusion.6), channel_id=1, source_target_pairs={{0,8},{4,12},{8,0},{12,4},{16,24},{20,28},{24,16},{28,20},{1,9},{5... | collective-permute-start | bytes 3145736 | tf_op jit(solution)/shard_map/ppermute | solution.py:90
  434.9 25.7 %slice-start = ((s8[8388608]{0:T(1024)(128)(4,1)}), s8[4194304]{0:T(1024)(128)(4,1)S(1)}, s32[]{:S(2)}) async-start(s8[8388608]{0:T(1024)(128)(4,1)} %bitcast.157), calls=%async_computation.5 | async-start | bytes 8388608
  435.0 47.3 %collective-permute-start.13 = (bf16[2,64,4096]{2,1,0:T(8,128)(2,1)S(1)}, bf16[2,64,4096]{2,1,0:T(8,128)(2,1)S(1)}, u32[]{:S(2)}, u32[]{:S(2)}) collective-permute-start(bf16[2,64,4096]{2,1,0:T(8,128)(2,1)S(1)} %pad_maximum_fusion.4), channel_id=1, source_target_pairs={{0,16},{4,20},{8,24},{12,28},{16,0},{20,4},{24,8},{28,12},{1,17},{... | collective-permute-start | bytes 3145736 | tf_op jit(solution)/shard_map/ppermute | solution.py:93
  437.2 23.4 %slice-start.1 = ((s8[8388608]{0:T(1024)(128)(4,1)}), s8[4194304]{0:T(1024)(128)(4,1)S(1)}, s32[]{:S(2)}) async-start(s8[8388608]{0:T(1024)(128)(4,1)} %bitcast.157), calls=%async_computation.6 | async-start | bytes 8388608
  437.2 45.6 %collective-permute-start.11 = (bf16[2,64,4096]{2,1,0:T(8,128)(2,1)S(1)}, bf16[2,64,4096]{2,1,0:T(8,128)(2,1)S(1)}, u32[]{:S(2)}, u32[]{:S(2)}) collective-permute-start(bf16[2,64,4096]{2,1,0:T(8,128)(2,1)S(1)} %pad_maximum_fusion.3), channel_id=1, source_target_pairs={{0,8},{4,12},{8,0},{12,4},{16,24},{20,28},{24,16},{28,20},{1,9},{5... | collective-permute-start | bytes 3145736 | tf_op jit(solution)/shard_map/ppermute | solution.py:90
  460.9 32.6 %collective-permute-start.17 = (bf16[256,1024]{1,0:T(8,128)(2,1)S(1)}, bf16[256,1024]{1,0:T(8,128)(2,1)S(1)}, u32[]{:S(2)}, u32[]{:S(2)}) collective-permute-start(bf16[256,1024]{1,0:T(8,128)(2,1)S(1)} %get-tuple-element.21), channel_id=1, source_target_pairs={{0,16},{4,20},{8,24},{12,28},{16,0},{20,4},{24,8},{28,12},{1,17},{... | collective-permute-start | bytes 1572872 | tf_op jit(solution)/shard_map/ppermute | solution.py:100
  462.6 31.4 %collective-permute-start.19 = (bf16[256,1024]{1,0:T(8,128)(2,1)S(1)}, bf16[256,1024]{1,0:T(8,128)(2,1)S(1)}, u32[]{:S(2)}, u32[]{:S(2)}) collective-permute-start(bf16[256,1024]{1,0:T(8,128)(2,1)S(1)} %get-tuple-element.22), channel_id=1, source_target_pairs={{0,8},{4,12},{8,0},{12,4},{16,24},{20,28},{24,16},{28,20},{1,9},{5... | collective-permute-start | bytes 1572872 | tf_op jit(solution)/shard_map/ppermute | solution.py:103
  483.3 18.3 %collective-permute-start.12 = (bf16[64,4096]{1,0:T(8,128)(2,1)S(1)}, bf16[64,4096]{1,0:T(8,128)(2,1)S(1)}, u32[]{:S(2)}, u32[]{:S(2)}) collective-permute-start(bf16[64,4096]{1,0:T(8,128)(2,1)S(1)} %get-tuple-element.27), channel_id=1, source_target_pairs={{0,16},{4,20},{8,24},{12,28},{16,0},{20,4},{24,8},{28,12},{1,17},{... | collective-permute-start | bytes 1572872 | tf_op jit(solution)/shard_map/ppermute | solution.py:100
  485.0 17.7 %collective-permute-start.14 = (bf16[64,4096]{1,0:T(8,128)(2,1)S(1)}, bf16[64,4096]{1,0:T(8,128)(2,1)S(1)}, u32[]{:S(2)}, u32[]{:S(2)}) collective-permute-start(bf16[64,4096]{1,0:T(8,128)(2,1)S(1)} %get-tuple-element.28), channel_id=1, source_target_pairs={{0,8},{4,12},{8,0},{12,4},{16,24},{20,28},{24,16},{28,20},{1,9},{5... | collective-permute-start | bytes 1572872 | tf_op jit(solution)/shard_map/ppermute | solution.py:103
  495.8 8.4 %copy-start.16 = (s32[512]{0:T(512)S(1)}, s32[512]{0:T(512)}, u32[]{:S(2)}) copy-start(s32[512]{0:T(512)} %param.14) | copy-start | bytes 6148
  495.8 8.4 %copy-start.27 = (f32[1,512]{1,0:T(1,128)S(1)}, f32[1,512]{1,0:T(1,128)}, u32[]{:S(2)}) copy-start(f32[1,512]{1,0:T(1,128)} %copy-done.26) | copy-start | bytes 6148
  504.2 10.1 %copy-start.5 = (f32[512,1024]{1,0:T(8,128)S(1)}, f32[512,1024]{1,0:T(8,128)}, u32[]{:S(2)}) copy-start(f32[512,1024]{1,0:T(8,128)} %get-tuple-element.18) | copy-start | bytes 6291460
  504.2 10.1 %copy-start.19 = (f32[1024]{0:T(1024)S(1)}, f32[1024]{0:T(1024)}, u32[]{:S(2)}) copy-start(f32[1024]{0:T(1024)} %convert_element_type.255) | copy-start | bytes 12292
  504.2 10.1 %copy-start.23 = (f32[8,1,128]{2,1,0:T(1,128)S(1)}, f32[8,1,128]{2,1,0:T(1,128)}, u32[]{:S(2)}) copy-start(f32[8,1,128]{2,1,0:T(1,128)} %copy-done.22) | copy-start | bytes 12292
  504.2 10.1 %copy-start.29 = (f32[512]{0:T(512)S(1)}, f32[512]{0:T(512)}, u32[]{:S(2)}) copy-start(f32[512]{0:T(512)} %copy-done.28) | copy-start | bytes 6148
  504.2 10.1 %copy-start.31 = (f32[512]{0:T(512)S(1)}, f32[512]{0:T(512)}, u32[]{:S(2)}) copy-start(f32[512]{0:T(512)} %copy-done.30) | copy-start | bytes 6148
  504.2 10.1 %copy-start.32 = (f32[512]{0:T(512)S(1)}, f32[512]{0:T(512)}, u32[]{:S(2)}) copy-start(f32[512]{0:T(512)} %multiply_multiply_fusion.2) | copy-start | bytes 6148
  504.2 10.1 %copy-start.35 = (f32[512]{0:T(512)S(1)}, f32[512]{0:T(512)}, u32[]{:S(2)}) copy-start(f32[512]{0:T(512)} %copy-done.33) | copy-start | bytes 6148
  504.2 10.1 %copy-start.37 = (f32[512]{0:T(512)S(1)}, f32[512]{0:T(512)}, u32[]{:S(2)}) copy-start(f32[512]{0:T(512)} %copy-done.36) | copy-start | bytes 6148
  504.2 10.1 %copy-start.42 = (f32[512,1024]{1,0:T(8,128)S(1)}, f32[512,1024]{1,0:T(8,128)}, u32[]{:S(2)}) copy-start(f32[512,1024]{1,0:T(8,128)} %get-tuple-element.67) | copy-start | bytes 6291460
  504.3 10.1 %copy-start.43 = (f32[512,1024]{1,0:T(8,128)S(1)}, f32[512,1024]{1,0:T(8,128)}, u32[]{:S(2)}) copy-start(f32[512,1024]{1,0:T(8,128)} %get-tuple-element.63) | copy-start | bytes 6291460
  623.6 7.1 %copy-start.10 = (bf16[512,1024]{1,0:T(8,128)(2,1)S(1)}, bf16[512,1024]{1,0:T(8,128)(2,1)}, u32[]{:S(2)}) copy-start(bf16[512,1024]{1,0:T(8,128)(2,1)} %get-tuple-element.16) | copy-start | bytes 3145732
  (9 other events, 22.9 us)
Sparse Core Ops, SparseCore 0:
  9.9 48.1 all-gather.6
  59.9 27.7 all-gather.8
  89.6 54.2 all-gather.10
  145.6 54.2 all-gather.12
  504.3 119.2 all-reduce.2
where the time goes:
time: 649 us; the launch traced here: 639 us
  waiting for transfers between devices  241 us (37%)
  matrix products  177 us (27%)
  other arithmetic  71.4 us (11%)
  blocking collectives  71.3 us (11%)
  local copies, waits for them, and re-layouts  43.3 us (7%)
  starting transfers between devices  20.8 us (3%)
  between operations  15.1 us (2%)
    psum x1, waiting for transfers between devices, plane_reduce(): return lax.psum(shard.astype(jnp.bfloat16), 'dp').astype(jnp.float32)  97.5 us
    psum x1, blocking collectives, per_device(): lax.psum(jnp.concatenate([grad_gain_one, grad_gain_two, router_local]), (...  52 us
    ppermute x4, waiting for transfers between devices, plane_reduce(): lax.ppermute(jnp.stack([to_y[half:], to_d[half:]]).astype(jnp.bfloat16),...  43.7 us
    all_gather x1, waiting for transfers between devices, per_device(): lax.all_gather(mlp_in, 'fsdp', axis=0, tiled=True)  38.6 us
    all_gather x1, waiting for transfers between devices, per_device(): w_down = lax.all_gather(mlp_out, 'fsdp', axis=0, tiled=True)  35.3 us
    add x4, other arithmetic, plane_reduce(): chip = keep + got.astype(jnp.float32)  20.5 us
    convert_element_type x4, local copies, waits for them, and re-layouts, plane_reduce(): got = lax.ppermute(send.astype(jnp.bfloat16), 'fsdp', swap_pairs(1, 8))  14.3 us
    dot_general x1, matrix products, per_device(): jnp.einsum('kd,fd->kf', grad_expanded, w_down, preferred_element_type=jnp...  13.3 us
  transfers between devices with their start and end apart: 25, of which 14 were waited for; matrix products, arithmetic and copies ran while one was open for 28% of the time, Pallas kernels for 0%

commit v1 on v0

--- a/solution.py
+++ b/solution.py
@@ -67,6 +67,10 @@
 
 
 def plane_reduce(grad):
+
+    def fill_domain(mat):
+        return lax.all_gather(mat, "dp").sum(axis=0)
+
     rows, cols = grad.shape
     part = rows // 8
     half = part // 2
@@ -104,7 +108,7 @@
         jnp.float32
     )
     shard = jnp.concatenate([own_a + second_y, own_b + second_x], axis=0)
-    return lax.psum(shard.astype(jnp.bfloat16), "dp").astype(jnp.float32)
+    return fill_domain(shard.astype(jnp.bfloat16)).astype(jnp.float32)
 
 
 def plain_reduce(grad):

time: 649 us -> 607 us (0.935)
  waiting for transfers between devices: 241 us -> 207 us
  blocking collectives: 71.3 us -> 63.2 us
  other arithmetic: 71.4 us -> 78.9 us
  local copies, waits for them, and re-layouts: 43.3 us -> 36.7 us
    psum x1 -> x0, waiting for transfers between devices: 97.5 us -> none  [plane_reduce(): return lax.psum(shard.astype(jnp.bfloat16), 'dp').astype(jnp.float32)]
    all_gather x0 -> x4, waiting for transfers between devices: none -> 53.7 us  [fill_domain(): return lax.all_gather(mat, 'dp').sum(axis=0)]
    reduce_sum x0 -> x4, other arithmetic: none -> 10.4 us  [fill_domain(): return lax.all_gather(mat, 'dp').sum(axis=0)]
    all_gather x1, waiting for transfers between devices: 35.3 us -> 44 us  [per_device(): w_down = lax.all_gather(mlp_out, 'fsdp', axis=0, tiled=True)]
    psum x1, blocking collectives: 52 us -> 43.9 us  [per_device(): lax.psum(jnp.concatenate([grad_gain_one, grad_gain_two, router_local]), (...]
    concatenate x4 -> x8, other arithmetic: 3.81 us -> 10.6 us  [plane_reduce(): shard = jnp.concatenate([own_a + second_y, own_b + second_x], axis=0)]
  transfers between devices with their start and end apart: 25 -> 28, of which waited for: 14 -> 15; matrix products, arithmetic and copies ran while one was open for 28% -> 33% of each run, Pallas kernels for 0% -> 0%
where the time goes in v1:
time: 607 us; the launch traced here: 598 us
  waiting for transfers between devices  207 us (34%)
  matrix products  179 us (29%)
  other arithmetic  78.9 us (13%)
  blocking collectives  63.2 us (10%)
  local copies, waits for them, and re-layouts  36.7 us (6%)
  starting transfers between devices  18.7 us (3%)
  between operations  15.1 us (2%)
    all_gather x4, waiting for transfers between devices, fill_domain(): return lax.all_gather(mat, 'dp').sum(axis=0)  53.7 us
    ppermute x4, waiting for transfers between devices, plane_reduce(): lax.ppermute(jnp.stack([to_y[half:], to_d[half:]]).astype(jnp.bfloat16),...  46.5 us
    all_gather x1, waiting for transfers between devices, per_device(): w_down = lax.all_gather(mlp_out, 'fsdp', axis=0, tiled=True)  44 us
    psum x1, blocking collectives, per_device(): lax.psum(jnp.concatenate([grad_gain_one, grad_gain_two, router_local]), (...  43.9 us
    all_gather x1, waiting for transfers between devices, per_device(): lax.all_gather(mlp_in, 'fsdp', axis=0, tiled=True)  38.7 us
    add x4, other arithmetic, plane_reduce(): chip = keep + got.astype(jnp.float32)  16.7 us
    dot_general x1, matrix products, per_device(): jnp.einsum('kd,fd->kf', grad_expanded, w_down, preferred_element_type=jnp...  14.6 us
    dot_general x1, matrix products, per_device(): jnp.einsum('qhd,khd->hqk', grad_mix_heads, value_heads, preferred_element...  12.8 us
  transfers between devices with their start and end apart: 28, of which 15 were waited for; matrix products, arithmetic and copies ran while one was open for 33% of the time, Pallas kernels for 0%

profile of v1, /device:TPU:0, one launch (start us, length us, event | category | flops | bytes accessed | tf_op | source)
XLA Modules:
  0.0 598.0 jit_solution(11290603815287356935)
XLA Ops:
  10.9 10.4 %all-gather = bf16[8,1,128]{2,1,0:T(2,128)(2,1)S(1)} all-gather(bf16[1,1,128]{2,1,0:T(2,128)(2,1)} %bitcast.224), channel_id=1, replica_groups=mesh['fsdp'=8,'dp'=4] {'fsdp'}, dimensions={0}, use_global_device_ids=true | all-gather | bytes 2304 | tf_op jit(solution)/shard_map/all_gather | solution.py:139
  21.3 8.9 %all-gather.1 = bf16[8,1,128]{2,1,0:T(2,128)(2,1)S(1)} all-gather(bf16[1,1,128]{2,1,0:T(2,128)(2,1)} %bitcast.225), channel_id=1, replica_groups=mesh['fsdp'=8,'dp'=4] {'fsdp'}, dimensions={0}, use_global_device_ids=true | all-gather | bytes 2304 | tf_op jit(solution)/shard_map/all_gather | solution.py:144
  31.7 8.0 %multiply_reduce_fusion.7 = (f32[512]{0:T(512)S(1)}, f32[512,1024]{1,0:T(8,128)S(1)}) fusion(bf16[4096,1024]{1,0:T(8,128)(2,1)} %param.11, s32[512]{0:T(512)} %param.14), kind=kOutput, calls=%fused_computation.64 | convolution fusion | flops 4298112512 | bytes 10489856 | tf_op jit(solution)/shard_map/dot_general | solution.py:151
  40.4 9.3 %fusion.12 = f32[512,1024]{1,0:T(8,128)} fusion(bf16[4096,1024]{1,0:T(8,128)(2,1)} %param.12, s32[512]{0:T(512)S(1)} %copy-done.22), kind=kOutput, calls=%fused_computation.28 | convolution fusion | flops 4297064448 | bytes 10487808 | tf_op jit(solution)/shard_map/dot_general | solution.py:185
  49.6 8.4 %all-gather.11.cloned.1.call-done = bf16[1024,3072]{1,0:T(8,128)(2,1)} async-done(((bf16[128,3072]{1,0:T(8,128)(2,1)}), bf16[1024,3072]{1,0:T(8,128)(2,1)}) %all-gather.11.cloned.1.call-update) | async-done | bytes 6291472 | tf_op jit(solution)/shard_map/all_gather | solution.py:138
  58.0 6.6 %convolution_convert_fusion = bf16[512,3072]{1,0:T(8,128)(2,1)S(1)} fusion(bf16[1024,3072]{1,0:T(8,128)(2,1)} %all-gather.11.cloned.1.call-done, f32[512,1024]{1,0:T(8,128)S(1)} %get-tuple-element.55, f32[1024]{0:T(1024)S(1)} %bitcast.210, f32[512]{0:T(512)S(1)} %fusion.92), kind=kOutput, calls=%fused_computation.34 | convolution fusion | flops 3224371200 | bytes 11540480 | tf_op jit(solution)/shard_map/dot_general | solution.py:157
  64.6 1.7 fusion.105
  66.4 1.5 copy.53
  67.9 2.3 copy.52
  70.2 2.3 copy.51
  72.4 8.8 %fusion.1 = (f32[16,512]{1,0:T(8,128)S(1)}, f32[16,512,512]{1,2,0:T(8,128)}) fusion(pred[512,512]{0,1:T(8,128)(4,1)S(1)} %compare_and_fusion, bf16[512,16,64]{0,2,1:T(8,128)(2,1)} %bitcast.191, bf16[512,16,64]{0,2,1:T(8,128)(2,1)S(1)} %bitcast.189), kind=kOutput, calls=%fused_computation.11 | convolution fusion | flops 549445632 | bytes 19169280 | tf_op jit(solution)/shard_map/qhd,khd->hqk/dot_general | solution.py:29
  81.3 9.3 %fusion = f32[16,512]{1,0:T(8,128)S(1)} fusion(f32[16,512,512]{1,2,0:T(8,128)} %get-tuple-element.57, f32[16,512]{1,0:T(8,128)S(1)} %get-tuple-element.56, pred[512,512]{0,1:T(8,128)(4,1)S(1)} %compare_and_fusion), kind=kLoop, calls=%fused_computation.8 | loop fusion | flops 16769024 | bytes 17104896 | tf_op jit(solution)/shard_map/reduce_sum | solution.py:164
  90.6 9.4 %fusion.26 = bf16[16,64,512]{2,1,0:T(8,128)(2,1)} fusion(bf16[512,16,64]{0,2,1:T(8,128)(2,1)} %bitcast.205, f32[16,512,512]{1,2,0:T(8,128)} %get-tuple-element.57, f32[16,512]{1,0:T(8,128)S(1)} %fusion, f32[16,512]{1,0:T(8,128)S(1)} %get-tuple-element.56, pred[512,512]{0,1:T(8,128)(4,1)S(1)} %compare_and_fusion), kind=kOutput, calls=%fused_computation.68 | convolution fusion | flops 558366720 | bytes 19202048 | tf_op jit(solution)/shard_map/hqk,khd->qhd/dot_general | solution.py:167
  100.0 5.2 multiply_reduce_fusion.6
  105.2 38.7 %all-gather.15.cloned.1.call-done = bf16[1024,4096]{1,0:T(8,128)(2,1)} async-done(((bf16[128,4096]{1,0:T(8,128)(2,1)}), bf16[1024,4096]{1,0:T(8,128)(2,1)}) %all-gather.15.cloned.1.call-update) | async-done | bytes 8388624 | tf_op jit(solution)/shard_map/all_gather | solution.py:143
  143.9 12.1 %fusion.104 = f32[512,4096]{1,0:T(8,128)} fusion(bf16[1024,4096]{1,0:T(8,128)(2,1)} %all-gather.15.cloned.1.call-done, f32[512,1024]{1,0:T(8,128)} %get-tuple-element.14, f32[1024]{0:T(1024)S(1)} %bitcast.214, f32[512]{0:T(512)S(1)} %fusion.93), kind=kOutput, calls=%fused_computation.189 | convolution fusion | flops 4296540160 | bytes 18880512 | tf_op jit(solution)/shard_map/dot_general | solution.py:175
  156.0 44.0 %all-gather.17.cloned.1.call-done = bf16[4096,1024]{1,0:T(8,128)(2,1)} async-done(((bf16[512,1024]{1,0:T(8,128)(2,1)}), bf16[4096,1024]{1,0:T(8,128)(2,1)}) %all-gather.17.cloned.1.call-update) | async-done | bytes 8388624 | tf_op jit(solution)/shard_map/all_gather | solution.py:146
  199.9 14.6 %fusion.8 = bf16[512,4096]{1,0:T(8,128)(2,1)} fusion(f32[512,4096]{1,0:T(8,128)} %fusion.104, bf16[4096,1024]{1,0:T(8,128)(2,1)} %all-gather.17.cloned.1.call-done, f32[512,1024]{1,0:T(8,128)} %fusion.12, f32[512]{0:T(512)S(1)} %bitcast.219), kind=kOutput, calls=%fused_computation.18 | convolution fusion | flops 4337958912 | bytes 23070720 | tf_op jit(solution)/shard_map/kd,fd->kf/dot_general | solution.py:193
  214.6 10.9 %multiply_reduce_fusion.1 = (f32[1024]{0:T(1024)S(1)}, f32[512]{0:T(512)S(1)}, f32[512,1024]{1,0:T(8,128)}) fusion(f32[512,1024]{1,0:T(8,128)S(1)} %copy-done.10, f32[512]{0:T(512)S(1)} %fusion.93, f32[1024]{0:T(1024)S(1)} %bitcast.215, bf16[512,4096]{1,0:T(8,128)(2,1)} %fusion.8, bf16[1024,4096]{1,0:T(8,128)(2,1)} %all-gather.15.cloned.1.call-done), kind=kOutput, calls=%fused_computation.49 | convolution fusion | flops 4298111488 | bytes 16789504 | tf_op jit(solution)/shard_map/kf,df->kd/dot_general | solution.py:202
  225.5 10.3 %multiply_reduce_fusion.3 = (f32[512]{0:T(512)S(1)}, bf16[512,1024]{1,0:T(8,128)(2,1)S(1)}, f32[512,1024]{1,0:T(8,128)}) fusion(f32[512,1024]{1,0:T(8,128)S(1)} %copy-done.30, f32[512,1024]{1,0:T(8,128)S(1)} %copy-done.10, f32[512]{0:T(512)S(1)} %multiply_multiply_fusion.3, f32[512]{0:T(512)S(1)} %fusion.93, f32[512,1024]{1,0:T(8,128)} %get-tuple-element.59, ...), kind=kOutput, calls=%fused_computation.54 | convolution fusion | flops 4319608320 | bytes 28323840 | tf_op jit(solution)/shard_map/dot_general | solution.py:178
  236.8 2.3 convolution_convert_fusion.1
  239.1 2.3 copy.55
  241.4 10.6 %fusion.27 = bf16[16,64,512]{2,1,0:T(8,128)(2,1)S(1)} fusion(bf16[512,16,64]{0,2,1:T(8,128)(2,1)} %bitcast.207, f32[16,512]{1,0:T(8,128)S(1)} %log_add_fusion, f32[16,512,512]{1,2,0:T(8,128)} %get-tuple-element.57, pred[512,512]{0,1:T(8,128)(4,1)S(1)} %compare_and_fusion), kind=kOutput, calls=%fused_computation.70 | convolution fusion | flops 558366720 | bytes 19169280 | tf_op jit(solution)/shard_map/hqk,qhd->khd/dot_general | solution.py:231
  252.0 12.8 %multiply_reduce_fusion = (f32[16,512]{1,0:T(8,128)S(1)}, f32[16,512,512]{1,2,0:T(8,128)}) fusion(f32[16,512]{1,0:T(8,128)S(1)} %log_add_fusion, f32[16,512,512]{1,2,0:T(8,128)} %get-tuple-element.57, pred[512,512]{0,1:T(8,128)(4,1)S(1)} %compare_and_fusion, bf16[512,16,64]{0,2,1:T(8,128)(2,1)S(1)} %bitcast.208, bf16[512,16,64]{0,2,1:T(8,128)(2,1)S(1)} %bitcast.206), kind=kOutput, calls=%fused_computation.2 | convolution fusion | flops 562028544 | bytes 35979264 | tf_op jit(solution)/shard_map/qhd,khd->hqk/dot_general | solution.py:217
  264.8 12.6 %multiply_convert_fusion = bf16[16,512,512]{1,2,0:T(8,128)(2,1)S(1)} fusion(f32[16,512,512]{1,2,0:T(8,128)} %get-tuple-element.62, f32[16,512]{1,0:T(8,128)S(1)} %get-tuple-element.61, f32[16,512]{1,0:T(8,128)S(1)} %log_add_fusion, f32[16,512,512]{1,2,0:T(8,128)} %get-tuple-element.57, pred[512,512]{0,1:T(8,128)(4,1)S(1)} %compare_and_fusion), kind=kLoop, calls=%fused_computation.1 | loop fusion | flops 29360128 | bytes 42270720 | tf_op jit(solution)/shard_map/convert_element_type | solution.py:221
  277.4 2.6 multiply_convert_fusion.2
  280.0 1.5 multiply_convert_fusion.3
  283.7 3.7 fusion.30
  287.5 2.4 fusion.22
  290.5 2.5 copy-done.6
  295.2 9.1 %fusion.101 = f32[4096,1024]{1,0:T(8,128)S(1)} fusion(f32[512,1024]{1,0:T(8,128)} %fusion.12, f32[512]{0:T(512)S(1)} %bitcast.221, f32[512,4096]{1,0:T(8,128)} %fusion.104), kind=kOutput, calls=%fused_computation.186 | convolution fusion | flops 4314890240 | bytes 27265024 | tf_op jit(solution)/shard_map/kf,kd->fd/dot_general | solution.py:189
  304.3 3.2 fusion.17
  307.7 1.6 collective-permute-start.7
  309.8 1.5 copy-done.4
  311.3 4.6 bitcast_add_fusion.2
  317.2 1.5 collective-permute-start.3
  321.6 8.2 %fusion.103 = f32[1024,4096]{1,0:T(8,128)} fusion(bf16[512,4096]{1,0:T(8,128)(2,1)S(1)} %copy-done.29, f32[512,1024]{1,0:T(8,128)S(1)} %copy-done.11, f32[1024]{0:T(1024)S(1)} %bitcast.217, f32[512]{0:T(512)S(1)} %fusion.93), kind=kOutput, calls=%fused_computation.188 | convolution fusion | flops 4296540160 | bytes 23074816 | tf_op jit(solution)/shard_map/kd,kf->df/dot_general | solution.py:198
  330.7 5.9 collective-permute-done.3
  340.1 2.9 fusion.77
  344.7 6.0 %fusion.16 = bf16[4,128,4096]{2,1,0:T(8,128)(2,1)} fusion(f32[4,2,128,4096]{3,2,1,0:T(8,128)} %bitcast.195, s32[]{:T(128)S(6)} %select_n.98), kind=kLoop, calls=%fused_computation.35 | loop fusion | bytes 8388612 | tf_op jit(solution)/shard_map/convert_element_type | solution.py:84
  350.8 2.0 collective-permute-done.2
  353.8 2.1 fusion.76
  356.9 6.0 %bitcast_add_fusion = f32[4,512,1024]{2,1,0:T(8,128)S(1)} fusion(bf16[4,512,1024]{2,1,0:T(8,128)(2,1)} %collective-permute-done.15, f32[4,2,512,1024]{3,2,1,0:T(8,128)} %bitcast.194, s32[]{:T(128)S(6)} %select_n.97), kind=kLoop, calls=%fused_computation.21 | loop fusion | flops 4194304 | bytes 20971524 | tf_op jit(solution)/shard_map/add | solution.py:85
  365.3 21.0 %collective-permute-done.18 = bf16[2,256,1024]{2,1,0:T(8,128)(2,1)S(1)} collective-permute-done((bf16[2,256,1024]{2,1,0:T(8,128)(2,1)S(1)}, bf16[2,256,1024]{2,1,0:T(8,128)(2,1)S(1)}, u32[]{:S(2)}, u32[]{:S(2)}) %collective-permute-start.18) | collective-permute-done | bytes 1048608 | tf_op jit(solution)/shard_map/ppermute | solution.py:97
  391.1 5.8 bitcast_add_fusion.1
  397.0 3.4 copy-done
  400.6 2.7 fusion.72
  404.9 1.7 dynamic-slice_convert_fusion.7
  407.8 1.7 collective-permute-start.11
  409.4 19.5 %collective-permute-done.13 = bf16[2,64,4096]{2,1,0:T(8,128)(2,1)S(1)} collective-permute-done((bf16[2,64,4096]{2,1,0:T(8,128)(2,1)S(1)}, bf16[2,64,4096]{2,1,0:T(8,128)(2,1)S(1)}, u32[]{:S(2)}, u32[]{:S(2)}) %collective-permute-start.13) | collective-permute-done | bytes 1048608 | tf_op jit(solution)/shard_map/ppermute | solution.py:97
  429.6 2.0 fusion.69
  431.6 1.5 collective-permute-start.12
  434.3 6.9 %collective-permute-done.12 = bf16[64,4096]{1,0:T(8,128)(2,1)S(1)} collective-permute-done((bf16[64,4096]{1,0:T(8,128)(2,1)S(1)}, bf16[64,4096]{1,0:T(8,128)(2,1)S(1)}, u32[]{:S(2)}, u32[]{:S(2)}) %collective-permute-start.12) | collective-permute-done | bytes 524320 | tf_op jit(solution)/shard_map/ppermute | solution.py:104
  442.3 2.0 fusion.68
  446.5 8.4 %multiply_reduce_fusion.2 = (f32[1024]{0:T(1024)S(1)}, f32[512]{0:T(512)S(1)}, f32[512,1024]{1,0:T(8,128)}) fusion(f32[512,1024]{1,0:T(8,128)S(1)} %get-tuple-element.55, f32[512]{0:T(512)S(1)} %fusion.92, f32[1024]{0:T(1024)S(1)} %bitcast.212, bf16[1024,3072]{1,0:T(8,128)(2,1)} %all-gather.11.cloned.1.call-done, bf16[512,1024]{0,1:T(8,128)(2,1)} %bitcast.229, ...), kind=kOutput, calls=%fused_computation.50 | convolution fusion | flops 3233806848 | bytes 13643776 | tf_op jit(solution)/shard_map/ke,de->kd/dot_general | solution.py:244
  454.9 43.9 %psum.7 = f32[3072]{0:T(1024)S(1)} all-reduce(f32[3072]{0:T(1024)S(1)} %pad_maximum_fusion.15), channel_id=1, replica_groups=mesh['fsdp'=8,'dp'=4] {'fsdp','dp'}, use_global_device_ids=true, to_apply=%region_16.17 | all-reduce | flops 3072 | bytes 24576 | tf_op jit(solution)/shard_map/psum | solution.py:254
  500.1 10.0 %add_convert_fusion.1 = bf16[4096,1024]{1,0:T(8,128)(2,1)} fusion(bf16[4096,1024]{1,0:T(8,128)(2,1)} %param.11, s32[512]{0:T(512)S(1)} %copy-done.23, f32[512,1024]{1,0:T(8,128)} %get-tuple-element.60, f32[512]{0:T(512)S(1)} %bitcast.222), kind=kOutput, calls=%fused_computation.4 | convolution fusion | flops 4310695936 | bytes 18878464 | tf_op jit(solution)/shard_map/kt,kd->td/dot_general | solution.py:183
  510.2 11.5 %add_convert_fusion = bf16[4096,1024]{1,0:T(8,128)(2,1)} fusion(bf16[4096,1024]{1,0:T(8,128)(2,1)} %param.12, s32[512]{0:T(512)S(1)} %copy-done.23, f32[512,1024]{1,0:T(8,128)S(1)} %get-tuple-element.55, f32[512,1024]{1,0:T(8,128)S(1)} %copy-done.31, f32[1024]{0:T(1024)S(1)} %convert_element_type.291, f32[512]{0:T(512)S(1)} %get-tuple-element.42, ...), kind=kOutput, calls=%fused_computation | convolution fusion | flops 4316987392 | bytes 25190400 | tf_op jit(solution)/shard_map/kt,kd->td/dot_general | solution.py:251
  524.0 2.5 reduce_sum.162
  527.8 3.3 reduce_sum.165
  531.1 1.6 convert_element_type.341
  532.7 53.7 %all-gather.23.cloned.1.call-done = bf16[4,128,4096]{2,1,0:T(8,128)(2,1)} async-done(((bf16[1,128,4096]{2,1,0:T(8,128)(2,1)}), bf16[4,128,4096]{2,1,0:T(8,128)(2,1)}) %all-gather.23.cloned.1.call-update) | async-done | bytes 4194320 | tf_op jit(solution)/shard_map/all_gather | solution.py:72
  586.4 3.1 reduce_sum.164
  589.4 1.5 convert_element_type.329
  (171 shorter events, 44.6 us)
Async XLA Ops:
  7.2 50.9 %all-gather.11.cloned.1.call-start = ((), (), s32[]{:S(2)}) async-start(), calls=%async_computation | async-start | bytes 7077888 | tf_op jit(solution)/shard_map/all_gather | solution.py:138
  7.9 92.1 %all-gather.13.cloned.1.call-start = ((), (), s32[]{:S(2)}) async-start(), calls=%async_computation.1 | async-start | bytes 2359296 | tf_op jit(solution)/shard_map/all_gather | solution.py:141
  8.7 135.2 %all-gather.15.cloned.1.call-start = ((), (), s32[]{:S(2)}) async-start(), calls=%async_computation.2 | async-start | bytes 9437184 | tf_op jit(solution)/shard_map/all_gather | solution.py:143
  9.4 190.5 %all-gather.17.cloned.1.call-start = ((), (), s32[]{:S(2)}) async-start(), calls=%async_computation.3 | async-start | bytes 9437184 | tf_op jit(solution)/shard_map/all_gather | solution.py:146
  10.0 511.7 %all-gather.21.cloned.1.call-start = ((), (), s32[]{:S(2)}) async-start(), calls=%async_computation.5 | async-start | bytes 1310720 | tf_op jit(solution)/shard_map/all_gather | solution.py:72
  31.7 8.0 %copy-start.22 = (s32[512]{0:T(512)S(1)}, s32[512]{0:T(512)}, u32[]{:S(2)}) copy-start(s32[512]{0:T(512)} %param.14) | copy-start | bytes 6148
  39.7 0.7 copy-start.25
  199.9 14.6 %copy-start.10 = (f32[512,1024]{1,0:T(8,128)S(1)}, f32[512,1024]{1,0:T(8,128)}, u32[]{:S(2)}) copy-start(f32[512,1024]{1,0:T(8,128)} %get-tuple-element.14) | copy-start | bytes 6291460
  214.6 10.9 %copy-start.13 = (f32[512,1024]{1,0:T(8,128)S(1)}, f32[512,1024]{1,0:T(8,128)}, u32[]{:S(2)}) copy-start(f32[512,1024]{1,0:T(8,128)} %get-tuple-element.58) | copy-start | bytes 6291460
  214.6 10.9 %copy-start.27 = (bf16[4096,1024]{1,0:T(8,128)(2,1)S(1)}, bf16[4096,1024]{1,0:T(8,128)(2,1)}, u32[]{:S(2)}) copy-start(bf16[4096,1024]{1,0:T(8,128)(2,1)} %all-gather.17.cloned.1.call-done) | copy-start | bytes 25165828
  214.6 10.9 %copy-start.30 = (f32[512,1024]{1,0:T(8,128)S(1)}, f32[512,1024]{1,0:T(8,128)}, u32[]{:S(2)}) copy-start(f32[512,1024]{1,0:T(8,128)} %fusion.12) | copy-start | bytes 6291460
  225.5 11.3 %copy-start.16 = (bf16[1024,1024]{1,0:T(8,128)(2,1)S(1)}, bf16[1024,1024]{1,0:T(8,128)(2,1)}, u32[]{:S(2)}) copy-start(bf16[1024,1024]{1,0:T(8,128)(2,1)} %all-gather.13.cloned.1.call-done) | copy-start | bytes 6291460
  235.8 1.0 copy-start.20
  241.4 10.6 %copy-start.18 = (bf16[512,1024]{0,1:T(8,128)(2,1)S(1)}, bf16[512,1024]{0,1:T(8,128)(2,1)}, u32[]{:S(2)}) copy-start(bf16[512,1024]{0,1:T(8,128)(2,1)} %copy.51) | copy-start | bytes 3145732
  241.4 10.6 %copy-start.19 = (bf16[512,1024]{0,1:T(8,128)(2,1)S(1)}, bf16[512,1024]{0,1:T(8,128)(2,1)}, u32[]{:S(2)}) copy-start(bf16[512,1024]{0,1:T(8,128)(2,1)} %copy.55) | copy-start | bytes 3145732
  252.0 31.8 %copy-start.28 = (bf16[16,64,512]{2,1,0:T(8,128)(2,1)}, bf16[16,64,512]{2,1,0:T(8,128)(2,1)S(1)}, u32[]{:S(2)}) copy-start(bf16[16,64,512]{2,1,0:T(8,128)(2,1)S(1)} %fusion.27) | copy-start | bytes 3145732
  264.8 12.6 %copy-start.3 = (bf16[512,1024]{0,1:T(8,128)(2,1)S(1)}, bf16[512,1024]{0,1:T(8,128)(2,1)}, u32[]{:S(2)}) copy-start(bf16[512,1024]{0,1:T(8,128)(2,1)} %copy.52) | copy-start | bytes 3145732
  280.0 3.7 copy-start.17
  280.0 1.6 copy-start.7
  280.0 1.9 copy-start.21
  281.5 6.0 copy-start.14
  283.4 6.7 %collective-permute-start.5 = (bf16[4,128,1024]{2,1,0:T(8,128)(2,1)S(1)}, bf16[4,128,1024]{2,1,0:T(8,128)(2,1)S(1)}, u32[]{:S(2)}, u32[]{:S(2)}) collective-permute-start(bf16[4,128,1024]{2,1,0:T(8,128)(2,1)S(1)} %fusion.32), channel_id=1, source_target_pairs={{0,4},{4,0},{8,12},{12,8},{16,20},{20,16},{24,28},{28,24},{1,5},{5... | collective-permute-start | bytes 3145736 | tf_op jit(solution)/shard_map/ppermute | solution.py:84
  287.5 5.5 copy-start.6
  289.9 21.4 %collective-permute-start = (bf16[4,128,3072]{2,1,0:T(8,128)(2,1)}, bf16[4,128,3072]{2,1,0:T(8,128)(2,1)}, u32[]{:S(2)}, u32[]{:S(2)}) collective-permute-start(bf16[4,128,3072]{2,1,0:T(8,128)(2,1)} %fusion.22), channel_id=1, source_target_pairs={{0,4},{4,0},{8,12},{12,8},{16,20},{20,16},{24,28},{28,24},{1,5},{5... | collective-permute-start | bytes 9437192 | tf_op jit(solution)/shard_map/ppermute | solution.py:84
  293.0 14.5 %collective-permute-start.8 = (bf16[2,64,1024]{2,1,0:T(8,128)(2,1)S(1)}, bf16[2,64,1024]{2,1,0:T(8,128)(2,1)S(1)}, u32[]{:S(2)}, u32[]{:S(2)}) collective-permute-start(bf16[2,64,1024]{2,1,0:T(8,128)(2,1)S(1)} %pad_maximum_fusion.13), channel_id=1, source_target_pairs={{0,16},{4,20},{8,24},{12,28},{16,0},{20,4},{24,8},{28,12},{1,17},{... | collective-permute-start | bytes 786440 | tf_op jit(solution)/shard_map/ppermute | solution.py:97
  294.2 13.3 %collective-permute-start.6 = (bf16[2,64,1024]{2,1,0:T(8,128)(2,1)S(1)}, bf16[2,64,1024]{2,1,0:T(8,128)(2,1)S(1)}, u32[]{:S(2)}, u32[]{:S(2)}) collective-permute-start(bf16[2,64,1024]{2,1,0:T(8,128)(2,1)S(1)} %pad_maximum_fusion.12), channel_id=1, source_target_pairs={{0,8},{4,12},{8,0},{12,4},{16,24},{20,28},{24,16},{28,20},{1,9},{5... | collective-permute-start | bytes 786440 | tf_op jit(solution)/shard_map/ppermute | solution.py:94
  304.3 7.0 %copy-start.4 = (f32[4096,1024]{1,0:T(8,128)}, f32[4096,1024]{1,0:T(8,128)S(1)}, u32[]{:S(2)}) copy-start(f32[4096,1024]{1,0:T(8,128)S(1)} %fusion.101) | copy-start | bytes 50331652
  307.5 49.4 %collective-permute-start.15 = (bf16[4,512,1024]{2,1,0:T(8,128)(2,1)}, bf16[4,512,1024]{2,1,0:T(8,128)(2,1)}, u32[]{:S(2)}, u32[]{:S(2)}) collective-permute-start(bf16[4,512,1024]{2,1,0:T(8,128)(2,1)} %fusion.17), channel_id=1, source_target_pairs={{0,4},{4,0},{8,12},{12,8},{16,20},{20,16},{24,28},{28,24},{1,5},{5... | collective-permute-start | bytes 12582920 | tf_op jit(solution)/shard_map/ppermute | solution.py:84
  307.7 22.1 %collective-permute-start.7 = (bf16[64,1024]{1,0:T(8,128)(2,1)S(1)}, bf16[64,1024]{1,0:T(8,128)(2,1)S(1)}, u32[]{:S(2)}, u32[]{:S(2)}) collective-permute-start(bf16[64,1024]{1,0:T(8,128)(2,1)S(1)} %get-tuple-element.38), channel_id=1, source_target_pairs={{0,16},{4,20},{8,24},{12,28},{16,0},{20,4},{24,8},{28,12},{1,17},{... | collective-permute-start | bytes 393224 | tf_op jit(solution)/shard_map/ppermute | solution.py:104
  309.3 20.5 %collective-permute-start.9 = (bf16[64,1024]{1,0:T(8,128)(2,1)S(1)}, bf16[64,1024]{1,0:T(8,128)(2,1)S(1)}, u32[]{:S(2)}, u32[]{:S(2)}) collective-permute-start(bf16[64,1024]{1,0:T(8,128)(2,1)S(1)} %get-tuple-element.39), channel_id=1, source_target_pairs={{0,8},{4,12},{8,0},{12,4},{16,24},{20,28},{24,16},{28,20},{1,9},{5... | collective-permute-start | bytes 393224 | tf_op jit(solution)/shard_map/ppermute | solution.py:107
  315.9 13.9 %copy-start.2 = (f32[4,128,3072]{2,1,0:T(8,128)}, f32[4,128,3072]{2,1,0:T(8,128)S(1)}, u32[]{:S(2)}) copy-start(f32[4,128,3072]{2,1,0:T(8,128)S(1)} %bitcast_add_fusion.2) | copy-start | bytes 18874372
  315.9 4.2 copy-start.11
  315.9 5.6 copy-start.29
  317.2 19.5 %collective-permute-start.3 = (bf16[2,64,3072]{2,1,0:T(8,128)(2,1)}, bf16[2,64,3072]{2,1,0:T(8,128)(2,1)}, u32[]{:S(2)}, u32[]{:S(2)}) collective-permute-start(bf16[2,64,3072]{2,1,0:T(8,128)(2,1)} %pad_maximum_fusion.10), channel_id=1, source_target_pairs={{0,16},{4,20},{8,24},{12,28},{16,0},{20,4},{24,8},{28,12},{1,17},{... | collective-permute-start | bytes 2359304 | tf_op jit(solution)/shard_map/ppermute | solution.py:97
  319.6 19.2 %collective-permute-start.1 = (bf16[2,64,3072]{2,1,0:T(8,128)(2,1)}, bf16[2,64,3072]{2,1,0:T(8,128)(2,1)}, u32[]{:S(2)}, u32[]{:S(2)}) collective-permute-start(bf16[2,64,3072]{2,1,0:T(8,128)(2,1)} %pad_maximum_fusion.9), channel_id=1, source_target_pairs={{0,8},{4,12},{8,0},{12,4},{16,24},{20,28},{24,16},{28,20},{1,9},{5... | collective-permute-start | bytes 2359304 | tf_op jit(solution)/shard_map/ppermute | solution.py:94
  330.6 193.3 %all-gather.19.cloned.1.call-start = ((), (), s32[]{:S(2)}) async-start(), calls=%async_computation.4 | async-start | bytes 3932160 | tf_op jit(solution)/shard_map/all_gather | solution.py:72
  337.9 2.1 copy-start.8
  340.1 2.9 copy-start.9
  343.0 9.8 %collective-permute-start.2 = (bf16[64,3072]{1,0:T(8,128)(2,1)}, bf16[64,3072]{1,0:T(8,128)(2,1)S(1)}, u32[]{:S(2)}, u32[]{:S(2)}) collective-permute-start(bf16[64,3072]{1,0:T(8,128)(2,1)} %get-tuple-element.29), channel_id=1, source_target_pairs={{0,16},{4,20},{8,24},{12,28},{16,0},{20,4},{24,8},{28,12},{1,17},{... | collective-permute-start | bytes 1179656 | tf_op jit(solution)/shard_map/ppermute | solution.py:104
  344.2 9.6 %collective-permute-start.4 = (bf16[64,3072]{1,0:T(8,128)(2,1)S(1)}, bf16[64,3072]{1,0:T(8,128)(2,1)S(1)}, u32[]{:S(2)}, u32[]{:S(2)}) collective-permute-start(bf16[64,3072]{1,0:T(8,128)(2,1)S(1)} %get-tuple-element.30), channel_id=1, source_target_pairs={{0,8},{4,12},{8,0},{12,4},{16,24},{20,28},{24,16},{28,20},{1,9},{5... | collective-permute-start | bytes 1179656 | tf_op jit(solution)/shard_map/ppermute | solution.py:107
  350.8 40.4 %collective-permute-start.10 = (bf16[4,128,4096]{2,1,0:T(8,128)(2,1)}, bf16[4,128,4096]{2,1,0:T(8,128)(2,1)}, u32[]{:S(2)}, u32[]{:S(2)}) collective-permute-start(bf16[4,128,4096]{2,1,0:T(8,128)(2,1)} %fusion.16), channel_id=1, source_target_pairs={{0,4},{4,0},{8,12},{12,8},{16,20},{20,16},{24,28},{28,24},{1,5},{5... | collective-permute-start | bytes 12582920 | tf_op jit(solution)/shard_map/ppermute | solution.py:84
  356.8 171.0 %all-gather.25.cloned.1.call-start = ((), (), s32[]{:S(2)}) async-start(), calls=%async_computation.7 | async-start | bytes 5242880 | tf_op jit(solution)/shard_map/all_gather | solution.py:72
  362.9 24.4 %copy-start.1 = (f32[4,512,1024]{2,1,0:T(8,128)}, f32[4,512,1024]{2,1,0:T(8,128)S(1)}, u32[]{:S(2)}) copy-start(f32[4,512,1024]{2,1,0:T(8,128)S(1)} %bitcast_add_fusion) | copy-start | bytes 25165828
  363.4 22.9 %collective-permute-start.18 = (bf16[2,256,1024]{2,1,0:T(8,128)(2,1)S(1)}, bf16[2,256,1024]{2,1,0:T(8,128)(2,1)S(1)}, u32[]{:S(2)}, u32[]{:S(2)}) collective-permute-start(bf16[2,256,1024]{2,1,0:T(8,128)(2,1)S(1)} %pad_maximum_fusion.7), channel_id=1, source_target_pairs={{0,16},{4,20},{8,24},{12,28},{16,0},{20,4},{24,8},{28,12},{1,17},{... | collective-permute-start | bytes 3145736 | tf_op jit(solution)/shard_map/ppermute | solution.py:97
  364.2 22.9 %collective-permute-start.16 = (bf16[2,256,1024]{2,1,0:T(8,128)(2,1)S(1)}, bf16[2,256,1024]{2,1,0:T(8,128)(2,1)S(1)}, u32[]{:S(2)}, u32[]{:S(2)}) collective-permute-start(bf16[2,256,1024]{2,1,0:T(8,128)(2,1)S(1)} %pad_maximum_fusion.6), channel_id=1, source_target_pairs={{0,8},{4,12},{8,0},{12,4},{16,24},{20,28},{24,16},{28,20},{1,9},{5... | collective-permute-start | bytes 3145736 | tf_op jit(solution)/shard_map/ppermute | solution.py:94
  387.3 3.8 copy-start.5
  388.7 11.8 %collective-permute-start.17 = (bf16[256,1024]{1,0:T(8,128)(2,1)}, bf16[256,1024]{1,0:T(8,128)(2,1)}, u32[]{:S(2)}, u32[]{:S(2)}) collective-permute-start(bf16[256,1024]{1,0:T(8,128)(2,1)} %get-tuple-element.17), channel_id=1, source_target_pairs={{0,16},{4,20},{8,24},{12,28},{16,0},{20,4},{24,8},{28,12},{1,17},{... | collective-permute-start | bytes 1572872 | tf_op jit(solution)/shard_map/ppermute | solution.py:104
  389.9 10.8 %collective-permute-start.19 = (bf16[256,1024]{1,0:T(8,128)(2,1)S(1)}, bf16[256,1024]{1,0:T(8,128)(2,1)}, u32[]{:S(2)}, u32[]{:S(2)}) collective-permute-start(bf16[256,1024]{1,0:T(8,128)(2,1)S(1)} %get-tuple-element.18), channel_id=1, source_target_pairs={{0,8},{4,12},{8,0},{12,4},{16,24},{20,28},{24,16},{28,20},{1,9},{5... | collective-permute-start | bytes 1572872 | tf_op jit(solution)/shard_map/ppermute | solution.py:107
  396.9 3.4 copy-start
  404.5 181.9 %all-gather.23.cloned.1.call-start = ((), (), s32[]{:S(2)}) async-start(), calls=%async_computation.6 | async-start | bytes 5242880 | tf_op jit(solution)/shard_map/all_gather | solution.py:72
  406.8 22.1 %collective-permute-start.13 = (bf16[2,64,4096]{2,1,0:T(8,128)(2,1)S(1)}, bf16[2,64,4096]{2,1,0:T(8,128)(2,1)S(1)}, u32[]{:S(2)}, u32[]{:S(2)}) collective-permute-start(bf16[2,64,4096]{2,1,0:T(8,128)(2,1)S(1)} %pad_maximum_fusion.4), channel_id=1, source_target_pairs={{0,16},{4,20},{8,24},{12,28},{16,0},{20,4},{24,8},{28,12},{1,17},{... | collective-permute-start | bytes 3145736 | tf_op jit(solution)/shard_map/ppermute | solution.py:97
  407.8 21.6 %collective-permute-start.11 = (bf16[2,64,4096]{2,1,0:T(8,128)(2,1)S(1)}, bf16[2,64,4096]{2,1,0:T(8,128)(2,1)S(1)}, u32[]{:S(2)}, u32[]{:S(2)}) collective-permute-start(bf16[2,64,4096]{2,1,0:T(8,128)(2,1)S(1)} %pad_maximum_fusion.3), channel_id=1, source_target_pairs={{0,8},{4,12},{8,0},{12,4},{16,24},{20,28},{24,16},{28,20},{1,9},{5... | collective-permute-start | bytes 3145736 | tf_op jit(solution)/shard_map/ppermute | solution.py:94
  429.6 15.8 %copy-start.24 = (bf16[1024]{0:T(1024)(128)(2,1)S(1)}, bf16[1024]{0:T(1024)(128)(2,1)}, u32[]{:S(2)}) copy-start(bf16[1024]{0:T(1024)(128)(2,1)} %param.21) | copy-start | bytes 6148
  431.6 14.9 %copy-start.15 = (bf16[16,64,512]{2,1,0:T(8,128)(2,1)S(1)}, bf16[16,64,512]{2,1,0:T(8,128)(2,1)}, u32[]{:S(2)}) copy-start(bf16[16,64,512]{2,1,0:T(8,128)(2,1)} %copy-done.14) | copy-start | bytes 3145732
  431.6 9.6 %collective-permute-start.12 = (bf16[64,4096]{1,0:T(8,128)(2,1)S(1)}, bf16[64,4096]{1,0:T(8,128)(2,1)S(1)}, u32[]{:S(2)}, u32[]{:S(2)}) collective-permute-start(bf16[64,4096]{1,0:T(8,128)(2,1)S(1)} %get-tuple-element.23), channel_id=1, source_target_pairs={{0,16},{4,20},{8,24},{12,28},{16,0},{20,4},{24,8},{28,12},{1,17},{... | collective-permute-start | bytes 1572872 | tf_op jit(solution)/shard_map/ppermute | solution.py:104
  433.1 9.2 %collective-permute-start.14 = (bf16[64,4096]{1,0:T(8,128)(2,1)S(1)}, bf16[64,4096]{1,0:T(8,128)(2,1)S(1)}, u32[]{:S(2)}, u32[]{:S(2)}) collective-permute-start(bf16[64,4096]{1,0:T(8,128)(2,1)S(1)} %get-tuple-element.24), channel_id=1, source_target_pairs={{0,8},{4,12},{8,0},{12,4},{16,24},{20,28},{24,16},{28,20},{1,9},{5... | collective-permute-start | bytes 1572872 | tf_op jit(solution)/shard_map/ppermute | solution.py:107
  446.5 53.6 %copy-start.26 = (f32[512]{0:T(512)S(1)}, f32[512]{0:T(512)}, u32[]{:S(2)}) copy-start(f32[512]{0:T(512)} %copy-done.25) | copy-start | bytes 6148
  446.5 53.6 %copy-start.23 = (s32[512]{0:T(512)S(1)}, s32[512]{0:T(512)}, u32[]{:S(2)}) copy-start(s32[512]{0:T(512)} %param.14) | copy-start | bytes 6148
  500.1 10.1 %copy-start.12 = (f32[512,1024]{1,0:T(8,128)S(1)}, f32[512,1024]{1,0:T(8,128)}, u32[]{:S(2)}) copy-start(f32[512,1024]{1,0:T(8,128)} %get-tuple-element.14) | copy-start | bytes 6291460
  500.1 10.1 %copy-start.31 = (f32[512,1024]{1,0:T(8,128)S(1)}, f32[512,1024]{1,0:T(8,128)}, u32[]{:S(2)}) copy-start(f32[512,1024]{1,0:T(8,128)} %get-tuple-element.63) | copy-start | bytes 6291460
  500.1 10.0 %copy-start.32 = (f32[512,1024]{1,0:T(8,128)S(1)}, f32[512,1024]{1,0:T(8,128)}, u32[]{:S(2)}) copy-start(f32[512,1024]{1,0:T(8,128)} %get-tuple-element.59) | copy-start | bytes 6291460
Sparse Core Ops, SparseCore 0:
  9.9 48.1 all-gather.10
  59.9 27.7 all-gather.12
  89.6 54.2 all-gather.14
  145.6 54.2 all-gather.16
  330.8 27.9 all-gather.20
  360.7 62.8 all-gather.18
  425.1 80.3 all-gather.24
  507.1 79.2 all-gather.22
